TPU v7x, 1024 devices: a whole 8x8x8 slice. The times are simulated.
1024 devices in a mesh: dp: 64 (over y, x), bytes: 16 (over z, core).
Axes of the slice: x: 8, y: 8, z: 8, core: 2. Of those that a mesh axis runs over, the one named last changes fastest.
Arguments:
- byte_queries: bfloat16 [64, 2048, 1024], P('dp', 'bytes'), may hold values from -48 to 48
- byte_keys: bfloat16 [64, 2048, 1024], P('dp', 'bytes'), may hold values from -6 to 6
- byte_values: bfloat16 [64, 2048, 1024], P('dp', 'bytes'), may hold values from -6 to 6
- patch_starts: int32 [64, 16, 12], P('dp', 'bytes'), may hold values from 0 to 128, as said below
- patch_proj: bfloat16 [1024, 4096], P('dp', 'bytes'), may hold values from -0.1875 to 0.1875
- latent_proj: bfloat16 [4096, 4096], P('bytes', 'dp'), may hold values from -0.09375 to 0.09375
- latent_cotangent: bfloat16 [64, 192, 4096], P('dp', 'bytes'), may hold values from -6 to 6
Outputs:
- latent_out: bfloat16 [64, 192, 4096], P('dp', 'bytes')
- pooled_grad: bfloat16 [64, 192, 1024], P('dp', 'bytes')
Inputs may be any that keep to these rules, and one draw needn't show every extreme that they name: `patch_starts`: per shard the first entry is 0, entries increase strictly while below 128 and the rest equal 128; a shard has 6 to 12 patches, and in every stream some shard has exactly 12.
All inputs are finite; a program needn't handle non-finite values.
Results may differ from a plain program's by a relative error of at most 0.025.
Values may be sent and summed in bfloat16 or wider, within the bound.
No kernel may reach another device: no remote copies, remote signals or barrier semaphores. Data moves between devices by JAX's collectives and lax.ppermute only.
A program may use at most 32 MiB of HBM per device.

v0:
```python
import math

import jax
import jax.numpy as jnp
from jax import lax
from jax.sharding import PartitionSpec as P

HEAD_L = 64


def shifted(shard, axis, by):
    devices = lax.axis_size(axis)
    pairs = [(i, i + by) for i in range(devices) if 0 <= i + by < devices]
    return lax.ppermute(shard, axis, pairs)


def per_device(
    byte_queries, byte_keys, byte_values, patch_starts, patch_proj, latent_proj, latent_cotangent
):
    rows = byte_queries.shape[1]
    width = byte_queries.shape[2]
    heads = width // HEAD_L
    group_size = math.gcd(heads, 4)
    groups = heads // group_size
    received = {}
    for reach in (2, 1):
        received[reach] = shifted((byte_keys, byte_values), "bytes", reach)
    keys_all = jnp.concatenate([received[2][0][0], received[1][0][0], byte_keys[0]], axis=0)
    values_all = jnp.concatenate([received[2][1][0], received[1][1][0], byte_values[0]], axis=0)
    query_groups = byte_queries[0].reshape(rows, groups, group_size, HEAD_L).transpose(1, 0, 2, 3)
    key_groups = keys_all.reshape(3 * rows, groups, group_size, HEAD_L).transpose(1, 0, 2, 3)
    value_group_list = values_all.reshape(3 * rows, groups, group_size, HEAD_L).transpose(
        1, 0, 2, 3
    )
    qpos = jnp.arange(rows, dtype=jnp.int32)[:, None] + 2 * rows
    kpos = jnp.arange(3 * rows, dtype=jnp.int32)[None, :]
    position = lax.axis_index("bytes")
    reachable = (kpos >= 2 * rows) | (kpos >= rows) & (position >= 1) | (position >= 2)
    allowed = (kpos <= qpos) & (kpos > qpos - 2 * rows) & reachable

    def attend(items):
        query, keys, values = items
        scores = jnp.einsum(
            "ihd,jhd->hij", query, keys, preferred_element_type=jnp.float32
        ) * HEAD_L ** (-0.5)
        scores = jnp.where(allowed[None], scores, -1e30)
        top = jnp.max(scores, axis=-1, keepdims=True)
        expo = jnp.exp(scores - top)
        weights = (expo / jnp.sum(expo, axis=-1, keepdims=True)).astype(jnp.bfloat16)
        mixed = jnp.einsum("hij,jhd->ihd", weights, values, preferred_element_type=jnp.float32)
        return mixed.astype(jnp.bfloat16)

    encoded = lax.map(attend, (query_groups, key_groups, value_group_list))
    encoded = encoded.transpose(1, 0, 2, 3).reshape(rows, width)
    starts = patch_starts[0, 0]
    nexts = jnp.concatenate([starts[1:], jnp.full((1,), rows, jnp.int32)])
    place = jnp.arange(rows, dtype=jnp.int32)[None, :]
    member = (place >= starts[:, None]) & (place < nexts[:, None])
    length = jnp.sum(member.astype(jnp.float32), axis=-1)
    summed = jnp.dot(member.astype(jnp.bfloat16), encoded, preferred_element_type=jnp.float32)
    pooled = (summed / jnp.maximum(length, 1.0)[:, None]).astype(jnp.bfloat16)
    valid = starts < rows
    proj_cols, latent_row_list = (
        lax.all_gather(patch_proj, "dp", axis=0, tiled=True),
        lax.all_gather(latent_proj, "dp", axis=1, tiled=True),
    )
    patches = lax.all_gather(pooled[None], "bytes", axis=1, tiled=True)
    hidden_in = jnp.dot(patches[0], proj_cols, preferred_element_type=jnp.float32)
    activation = jax.nn.silu(hidden_in).astype(jnp.bfloat16)
    piece = activation
    latent = lax.psum_scatter(
        jnp.dot(piece, latent_row_list, preferred_element_type=jnp.float32).astype(jnp.bfloat16),
        "bytes",
        scatter_dimension=0,
        tiled=True,
    )
    cot_all = lax.all_gather(latent_cotangent, "bytes", axis=1, tiled=True)
    back = lax.dot_general(
        cot_all[0], latent_row_list, (((1,), (1,)), ((), ())), preferred_element_type=jnp.float32
    )
    sigma = jax.nn.sigmoid(hidden_in)
    act_grad = (back * sigma * (1.0 + hidden_in * (1.0 - sigma))).astype(jnp.bfloat16)
    piece = act_grad
    grads = lax.psum_scatter(
        lax.dot_general(
            piece, proj_cols, (((1,), (1,)), ((), ())), preferred_element_type=jnp.float32
        ).astype(jnp.bfloat16),
        "bytes",
        scatter_dimension=0,
        tiled=True,
    ).astype(jnp.float32)
    grads = jnp.where(valid[:, None], grads, 0.0)
    return (latent[None], grads.astype(jnp.bfloat16)[None])


def solution(mesh):
    return jax.shard_map(
        per_device,
        mesh=mesh,
        in_specs=(
            P("dp", "bytes", None),
            P("dp", "bytes", None),
            P("dp", "bytes", None),
            P("dp", "bytes", None),
            P("dp", "bytes"),
            P("bytes", "dp"),
            P("dp", "bytes", None),
        ),
        out_specs=(P("dp", "bytes", None), P("dp", "bytes", None)),
        check_vma=False,
    )
```

profile of v0, /device:TPU:131, one launch (start us, length us, event | category | flops | bytes accessed | tf_op | source)
XLA Modules:
  0.0 235.4 jit_solution(14656458523155805221)
XLA Ops:
  8.0 4.9 %collective-permute-start = (bf16[1,128,1024]{2,1,0:T(8,128)(2,1)}, bf16[1,128,1024]{2,1,0:T(8,128)(2,1)S(1)}, u32[]{:S(2)}, u32[]{:S(2)}) collective-permute-start(bf16[1,128,1024]{2,1,0:T(8,128)(2,1)} %param.11), channel_id=1, source_target_pairs={{0,2},{1,3},{2,4},{3,5},{4,6},{5,7},{6,8},{7,9},{8,10},{9,11},{10,... | collective-permute-start | bytes 786440 | tf_op jit(solution)/shard_map/ppermute | solution.py:14
  12.9 5.8 %collective-permute-start.1 = (bf16[1,128,1024]{2,1,0:T(8,128)(2,1)}, bf16[1,128,1024]{2,1,0:T(8,128)(2,1)S(1)}, u32[]{:S(2)}, u32[]{:S(2)}) collective-permute-start(bf16[1,128,1024]{2,1,0:T(8,128)(2,1)} %param.11), channel_id=1, source_target_pairs={{0,1},{1,2},{2,3},{3,4},{4,5},{5,6},{6,7},{7,8},{8,9},{9,10},{10,1... | collective-permute-start | bytes 786440 | tf_op jit(solution)/shard_map/ppermute | solution.py:14
  18.6 6.1 %collective-permute-start.2 = (bf16[1,128,1024]{2,1,0:T(8,128)(2,1)}, bf16[1,128,1024]{2,1,0:T(8,128)(2,1)S(1)}, u32[]{:S(2)}, u32[]{:S(2)}) collective-permute-start(bf16[1,128,1024]{2,1,0:T(8,128)(2,1)} %param.10), channel_id=1, source_target_pairs={{0,2},{1,3},{2,4},{3,5},{4,6},{5,7},{6,8},{7,9},{8,10},{9,11},{10,... | collective-permute-start | bytes 786440 | tf_op jit(solution)/shard_map/ppermute | solution.py:14
  24.8 2.2 collective-permute-start.3
  27.0 1.7 copy.46
  28.8 0.7 slice_bitcast_fusion
  29.5 41.4 %all_gather.13 = bf16[1024,256]{1,0:T(8,128)(2,1)S(1)} all-gather(bf16[16,256]{1,0:T(8,128)(2,1)} %param.13), channel_id=1, replica_groups=mesh['dp'=64,'bytes'=16] {'dp'}, dimensions={0}, use_global_device_ids=true | all-gather | bytes 532480 | tf_op jit(solution)/shard_map/all_gather | solution.py:64
  71.0 0.8 convert_reduce_fusion
  71.8 1.1 copy.45
  72.9 1.1 copy.41
  75.0 1.2 maximum_bitcast_fusion
  76.2 11.7 %while.11 = (s32[]{:T(128)}, bf16[4,128,4,64]{1,3,2,0:T(8,128)(2,1)S(1)}, bf16[4,384,4,64]{1,3,2,0:T(8,128)(2,1)}, bf16[4,128,4,64]{1,3,2,0:T(8,128)(2,1)S(1)}, ...) while((s32[]{:T(128)}, ...), condition=%wide.region_3.4_spmd.clone, body=%wide.region_0.3_spmd.clone.sunk | while | flops 77497600 | bytes 3301333 | solution.py:53
  77.1 2.0 fusion.95
  80.0 2.0 fusion.95
  83.0 2.0 fusion.95
  85.9 2.0 fusion.95
  88.1 27.8 %all-gather.1 = bf16[16,12,1024]{2,1,0:T(8,128)(2,1)S(1)} all-gather(bf16[1,12,1024]{2,1,0:T(8,128)(2,1)S(1)} %fusion.46), channel_id=2, replica_groups=mesh['dp'=64,'bytes'=16] {'bytes'}, dimensions={0}, use_global_device_ids=true | all-gather | bytes 417792 | tf_op jit(solution)/shard_map/all_gather | solution.py:67
  116.3 2.4 %convolution_convert_fusion.1 = bf16[192,4096]{1,0:T(8,128)(2,1)S(1)} fusion(bf16[256,4096]{0,1:T(8,128)(2,1)} %all-gather.5.cloned.1.call-done, f32[192,256]{1,0:T(8,128)S(1)} %fusion.68), kind=kOutput, calls=%fused_computation.28 | convolution fusion | flops 403685376 | bytes 3866624 | tf_op jit(solution)/shard_map/dot_general | solution.py:72
  118.8 40.3 %all-gather.7.cloned.1.call-done = bf16[1,192,4096]{2,0,1:T(2,128)(2,1)} async-done(((bf16[1,12,4096]{2,0,1:T(2,128)(2,1)}), bf16[1,192,4096]{2,0,1:T(2,128)(2,1)}) %all-gather.7.cloned.1.call-update) | async-done | bytes 1572880 | tf_op jit(solution)/shard_map/all_gather | solution.py:77
  159.1 4.7 %convolution_convert_fusion.2 = bf16[192,1024]{1,0:T(8,128)(2,1)S(1)} fusion(bf16[1024,256]{1,0:T(8,128)(2,1)S(1)} %all_gather.13, bf16[256,4096]{0,1:T(8,128)(2,1)} %all-gather.5.cloned.1.call-done, bf16[1,192,4096]{2,0,1:T(2,128)(2,1)} %all-gather.7.cloned.1.call-done, f32[192,256]{1,0:T(8,128)S(1)} %fusion.68), kind=kOutput, calls=%fused_computation.32 | convolution fusion | flops 503955456 | bytes 4784128 | tf_op jit(solution)/shard_map/dot_general | solution.py:85
  163.8 27.4 %fusion.62 = (bf16[16,4096]{1,0:T(8,128)(2,1)S(1)}, bf16[16,1024]{1,0:T(8,128)(2,1)S(1)}) fusion(bf16[192,4096]{1,0:T(8,128)(2,1)S(1)} %convolution_convert_fusion.1, bf16[192,1024]{1,0:T(8,128)(2,1)S(1)} %convolution_convert_fusion.2), kind=kCustom, calls=%all-reduce-scatter.2 | all-reduce-scatter fusion | flops 1310721 | bytes 2134016
  191.2 5.4 %collective-permute-start.10 = (bf16[16,1024]{1,0:T(8,128)(2,1)S(1)}, bf16[16,1024]{1,0:T(8,128)(2,1)S(1)}, u32[]{:S(2)}, u32[]{:S(2)}) collective-permute-start(bf16[16,1024]{1,0:T(8,128)(2,1)S(1)} %get-tuple-element.70), channel_id=1, source_target_pairs={{0,3},{1,4},{2,5},{3,6},{4,7},{5,8},{6,9},{7,10},{8,11},{9,12},{10... | collective-permute-start | bytes 98312
  196.6 3.6 %collective-permute-start.8 = (bf16[16,1024]{1,0:T(8,128)(2,1)S(1)}, bf16[16,1024]{1,0:T(8,128)(2,1)S(1)}, u32[]{:S(2)}, u32[]{:S(2)}) collective-permute-start(bf16[16,1024]{1,0:T(8,128)(2,1)S(1)} %get-tuple-element.70), channel_id=1, source_target_pairs={{0,1},{1,2},{2,3},{3,4},{4,5},{5,6},{6,7},{7,8},{8,9},{9,10},{10,1... | collective-permute-start | bytes 98312
  200.2 4.9 %collective-permute-start.9 = (bf16[16,1024]{1,0:T(8,128)(2,1)S(1)}, bf16[16,1024]{1,0:T(8,128)(2,1)S(1)}, u32[]{:S(2)}, u32[]{:S(2)}) collective-permute-start(bf16[16,1024]{1,0:T(8,128)(2,1)S(1)} %get-tuple-element.70), channel_id=1, source_target_pairs={{0,2},{1,3},{2,4},{3,5},{4,6},{5,7},{6,8},{7,9},{8,10},{9,11},{10,... | collective-permute-start | bytes 98312
  205.2 1.9 collective-permute-start.11
  207.1 1.3 dynamic-slice.6
  209.1 2.3 collective-permute-start.4
  211.4 2.1 collective-permute-start.5
  213.5 3.8 %collective-permute-start.6 = (bf16[16,4096]{1,0:T(8,128)(2,1)S(1)}, bf16[16,4096]{1,0:T(8,128)(2,1)S(1)}, u32[]{:S(2)}, u32[]{:S(2)}) collective-permute-start(bf16[16,4096]{1,0:T(8,128)(2,1)S(1)} %get-tuple-element.69), channel_id=1, source_target_pairs={{0,3},{1,4},{2,5},{3,6},{4,7},{5,8},{6,9},{7,10},{8,11},{9,12},{10... | collective-permute-start | bytes 393224
  217.3 1.6 collective-permute-start.7
  220.2 6.4 %collective-permute-done.7 = bf16[12,4096]{1,0:T(8,128)(2,1)S(1)} collective-permute-done((bf16[12,4096]{1,0:T(8,128)(2,1)S(1)}, bf16[12,4096]{1,0:T(8,128)(2,1)S(1)}, u32[]{:S(2)}, u32[]{:S(2)}) %collective-permute-start.7) | collective-permute-done | bytes 98336
  226.6 1.2 concatenate.32
  (51 shorter events, 8.1 us)
Async XLA Ops:
  7.2 66.9 %copy-start = (bf16[1,128,1024]{2,1,0:T(8,128)(2,1)S(1)}, bf16[1,128,1024]{2,1,0:T(8,128)(2,1)}, u32[]{:S(2)}) copy-start(bf16[1,128,1024]{2,1,0:T(8,128)(2,1)} %param.9) | copy-start | bytes 786436
  7.2 109.1 %all-gather.5.cloned.1.call-start = ((), (), s32[]{:S(2)}) async-start(), calls=%async_computation | async-start | bytes 2129920 | tf_op jit(solution)/shard_map/all_gather | solution.py:65
  7.9 151.1 %all-gather.7.cloned.1.call-start = ((), (), s32[]{:S(2)}) async-start(), calls=%async_computation.1 | async-start | bytes 3342336 | tf_op jit(solution)/shard_map/all_gather | solution.py:77
  8.0 66.3 %collective-permute-start = (bf16[1,128,1024]{2,1,0:T(8,128)(2,1)}, bf16[1,128,1024]{2,1,0:T(8,128)(2,1)S(1)}, u32[]{:S(2)}, u32[]{:S(2)}) collective-permute-start(bf16[1,128,1024]{2,1,0:T(8,128)(2,1)} %param.11), channel_id=1, source_target_pairs={{0,2},{1,3},{2,4},{3,5},{4,6},{5,7},{6,8},{7,9},{8,10},{9,11},{10,... | collective-permute-start | bytes 786440 | tf_op jit(solution)/shard_map/ppermute | solution.py:14
  12.9 61.6 %collective-permute-start.1 = (bf16[1,128,1024]{2,1,0:T(8,128)(2,1)}, bf16[1,128,1024]{2,1,0:T(8,128)(2,1)S(1)}, u32[]{:S(2)}, u32[]{:S(2)}) collective-permute-start(bf16[1,128,1024]{2,1,0:T(8,128)(2,1)} %param.11), channel_id=1, source_target_pairs={{0,1},{1,2},{2,3},{3,4},{4,5},{5,6},{6,7},{7,8},{8,9},{9,10},{10,1... | collective-permute-start | bytes 786440 | tf_op jit(solution)/shard_map/ppermute | solution.py:14
  18.6 56.0 %collective-permute-start.2 = (bf16[1,128,1024]{2,1,0:T(8,128)(2,1)}, bf16[1,128,1024]{2,1,0:T(8,128)(2,1)S(1)}, u32[]{:S(2)}, u32[]{:S(2)}) collective-permute-start(bf16[1,128,1024]{2,1,0:T(8,128)(2,1)} %param.10), channel_id=1, source_target_pairs={{0,2},{1,3},{2,4},{3,5},{4,6},{5,7},{6,8},{7,9},{8,10},{9,11},{10,... | collective-permute-start | bytes 786440 | tf_op jit(solution)/shard_map/ppermute | solution.py:14
  24.8 50.1 %collective-permute-start.3 = (bf16[1,128,1024]{2,1,0:T(8,128)(2,1)}, bf16[1,128,1024]{2,1,0:T(8,128)(2,1)S(1)}, u32[]{:S(2)}, u32[]{:S(2)}) collective-permute-start(bf16[1,128,1024]{2,1,0:T(8,128)(2,1)} %param.10), channel_id=1, source_target_pairs={{0,1},{1,2},{2,3},{3,4},{4,5},{5,6},{6,7},{7,8},{8,9},{9,10},{10,1... | collective-permute-start | bytes 786440 | tf_op jit(solution)/shard_map/ppermute | solution.py:14
  76.2 11.7 %copy-start.1 = (s32[1,1,12]{2,1,0:T(1,128)S(1)}, s32[1,1,12]{2,1,0:T(1,128)}, u32[]{:S(2)}) copy-start(s32[1,1,12]{2,1,0:T(1,128)} %param.12) | copy-start | bytes 148
  191.2 22.3 %collective-permute-start.10 = (bf16[16,1024]{1,0:T(8,128)(2,1)S(1)}, bf16[16,1024]{1,0:T(8,128)(2,1)S(1)}, u32[]{:S(2)}, u32[]{:S(2)}) collective-permute-start(bf16[16,1024]{1,0:T(8,128)(2,1)S(1)} %get-tuple-element.70), channel_id=1, source_target_pairs={{0,3},{1,4},{2,5},{3,6},{4,7},{5,8},{6,9},{7,10},{8,11},{9,12},{10... | collective-permute-start | bytes 98312
  196.6 20.7 %collective-permute-start.8 = (bf16[16,1024]{1,0:T(8,128)(2,1)S(1)}, bf16[16,1024]{1,0:T(8,128)(2,1)S(1)}, u32[]{:S(2)}, u32[]{:S(2)}) collective-permute-start(bf16[16,1024]{1,0:T(8,128)(2,1)S(1)} %get-tuple-element.70), channel_id=1, source_target_pairs={{0,1},{1,2},{2,3},{3,4},{4,5},{5,6},{6,7},{7,8},{8,9},{9,10},{10,1... | collective-permute-start | bytes 98312
  200.2 18.7 %collective-permute-start.9 = (bf16[16,1024]{1,0:T(8,128)(2,1)S(1)}, bf16[16,1024]{1,0:T(8,128)(2,1)S(1)}, u32[]{:S(2)}, u32[]{:S(2)}) collective-permute-start(bf16[16,1024]{1,0:T(8,128)(2,1)S(1)} %get-tuple-element.70), channel_id=1, source_target_pairs={{0,2},{1,3},{2,4},{3,5},{4,6},{5,7},{6,8},{7,9},{8,10},{9,11},{10,... | collective-permute-start | bytes 98312
  205.2 6.2 %collective-permute-start.11 = (bf16[12,1024]{1,0:T(8,128)(2,1)S(1)}, bf16[12,1024]{1,0:T(8,128)(2,1)S(1)}, u32[]{:S(2)}, u32[]{:S(2)}) collective-permute-start(bf16[12,1024]{1,0:T(8,128)(2,1)S(1)} %slice.9), channel_id=1, source_target_pairs={{0,4},{1,5},{2,6},{3,7},{4,8},{5,9},{6,10},{7,11},{8,12},{9,13},{1... | collective-permute-start | bytes 73736
  209.1 17.6 %collective-permute-start.4 = (bf16[16,4096]{1,0:T(8,128)(2,1)S(1)}, bf16[16,4096]{1,0:T(8,128)(2,1)S(1)}, u32[]{:S(2)}, u32[]{:S(2)}) collective-permute-start(bf16[16,4096]{1,0:T(8,128)(2,1)S(1)} %get-tuple-element.69), channel_id=1, source_target_pairs={{0,1},{1,2},{2,3},{3,4},{4,5},{5,6},{6,7},{7,8},{8,9},{9,10},{10,1... | collective-permute-start | bytes 393224
  211.4 15.2 %collective-permute-start.5 = (bf16[16,4096]{1,0:T(8,128)(2,1)S(1)}, bf16[16,4096]{1,0:T(8,128)(2,1)S(1)}, u32[]{:S(2)}, u32[]{:S(2)}) collective-permute-start(bf16[16,4096]{1,0:T(8,128)(2,1)S(1)} %get-tuple-element.69), channel_id=1, source_target_pairs={{0,2},{1,3},{2,4},{3,5},{4,6},{5,7},{6,8},{7,9},{8,10},{9,11},{10,... | collective-permute-start | bytes 393224
  213.5 13.1 %collective-permute-start.6 = (bf16[16,4096]{1,0:T(8,128)(2,1)S(1)}, bf16[16,4096]{1,0:T(8,128)(2,1)S(1)}, u32[]{:S(2)}, u32[]{:S(2)}) collective-permute-start(bf16[16,4096]{1,0:T(8,128)(2,1)S(1)} %get-tuple-element.69), channel_id=1, source_target_pairs={{0,3},{1,4},{2,5},{3,6},{4,7},{5,8},{6,9},{7,10},{8,11},{9,12},{10... | collective-permute-start | bytes 393224
  217.3 9.3 %collective-permute-start.7 = (bf16[12,4096]{1,0:T(8,128)(2,1)S(1)}, bf16[12,4096]{1,0:T(8,128)(2,1)S(1)}, u32[]{:S(2)}, u32[]{:S(2)}) collective-permute-start(bf16[12,4096]{1,0:T(8,128)(2,1)S(1)} %slice.8), channel_id=1, source_target_pairs={{0,4},{1,5},{2,6},{3,7},{4,8},{5,9},{6,10},{7,11},{8,12},{9,13},{1... | collective-permute-start | bytes 294920
Sparse Core Ops, SparseCore 0:
  12.2 94.2 all-gather.4
  109.2 49.7 all-gather.6
where the time goes:
time: 236 us; the launch traced here: 235 us
  blocking collectives  96.6 us (41%)
  waiting for transfers between devices  47.5 us (20%)
  starting transfers between devices  44.7 us (19%)
  matrix products  18.8 us (8%)
  between operations  15.1 us (6%)
  local copies, waits for them, and re-layouts  9.49 us (4%)
  other arithmetic  3.2 us (1%)
    all_gather x1, blocking collectives, per_device(): lax.all_gather(patch_proj, 'dp', axis=0, tiled=True)  41.4 us
    all_gather x1, waiting for transfers between devices, per_device(): cot_all = lax.all_gather(latent_cotangent, 'bytes', axis=1, tiled=True)  40.3 us
    all_gather x1, blocking collectives, per_device(): patches = lax.all_gather(pooled[None], 'bytes', axis=1, tiled=True)  27.8 us
    unnamed x1, blocking collectives  27.4 us
    unnamed x8, starting transfers between devices  25.6 us
    ppermute x4, starting transfers between devices, shifted(): return lax.ppermute(shard, axis, pairs)  19 us
    dot_general x4, matrix products, attend(): jnp.einsum('hij,jhd->ihd', weights, values, preferred_element_type=jnp.fl...  7.92 us
    unnamed x14, local copies, waits for them, and re-layouts  7.39 us
  transfers between devices with their start and end apart: 14, of which 2 were waited for; matrix products, arithmetic and copies ran while one was open for 11% of the time, Pallas kernels for 0%

commit v1 on v0

v1 whole, which is shorter than its diff:
```python
import math

import jax
import jax.numpy as jnp
import numpy as np
from jax import lax
from jax.sharding import Mesh
from jax.sharding import PartitionSpec as P

HEAD_L = 64
BYTE_AXES = ("z", "c")
DP_AXES = ("y", "x")


def shifted(shard, axis, by):
    devices = lax.axis_size(axis)
    pairs = [(i, i + by) for i in range(devices) if 0 <= i + by < devices]
    return lax.ppermute(shard, axis, pairs)


def per_device(
    byte_queries, byte_keys, byte_values, patch_starts, patch_proj, latent_proj, latent_cotangent
):
    rows = byte_queries.shape[1]
    width = byte_queries.shape[2]
    heads = width // HEAD_L
    group_size = math.gcd(heads, 4)
    groups = heads // group_size

    proj_rows, block = patch_proj.shape
    lat_rows, lat_cols = latent_proj.shape
    wbuf = jnp.concatenate([patch_proj.reshape(-1), latent_proj.reshape(-1)])
    wbuf = lax.all_gather(wbuf, "x", axis=0)
    wbuf = lax.all_gather(wbuf, "y", axis=0)
    ndp = wbuf.shape[0] * wbuf.shape[1]
    wbuf = wbuf.reshape(ndp, -1)
    proj_cols = wbuf[:, : proj_rows * block].reshape(ndp * proj_rows, block)
    latent_w = wbuf[:, proj_rows * block :].reshape(ndp, lat_rows, lat_cols)

    cot = lax.all_gather(latent_cotangent[0], "z", axis=0, tiled=True)
    cot_all = lax.all_gather(cot, "c", axis=0, tiled=True)

    received = {}
    for reach in (2, 1):
        received[reach] = shifted((byte_keys, byte_values), BYTE_AXES, reach)
    keys_all = jnp.concatenate([received[2][0][0], received[1][0][0], byte_keys[0]], axis=0)
    values_all = jnp.concatenate([received[2][1][0], received[1][1][0], byte_values[0]], axis=0)
    query_groups = byte_queries[0].reshape(rows, groups, group_size, HEAD_L).transpose(1, 0, 2, 3)
    key_groups = keys_all.reshape(3 * rows, groups, group_size, HEAD_L).transpose(1, 0, 2, 3)
    value_group_list = values_all.reshape(3 * rows, groups, group_size, HEAD_L).transpose(
        1, 0, 2, 3
    )
    qpos = jnp.arange(rows, dtype=jnp.int32)[:, None] + 2 * rows
    kpos = jnp.arange(3 * rows, dtype=jnp.int32)[None, :]
    position = lax.axis_index(BYTE_AXES)
    reachable = (kpos >= 2 * rows) | (kpos >= rows) & (position >= 1) | (position >= 2)
    allowed = (kpos <= qpos) & (kpos > qpos - 2 * rows) & reachable

    def attend(items):
        query, keys, values = items
        scores = jnp.einsum(
            "ihd,jhd->hij", query, keys, preferred_element_type=jnp.float32
        ) * HEAD_L ** (-0.5)
        scores = jnp.where(allowed[None], scores, -1e30)
        top = jnp.max(scores, axis=-1, keepdims=True)
        expo = jnp.exp(scores - top)
        weights = (expo / jnp.sum(expo, axis=-1, keepdims=True)).astype(jnp.bfloat16)
        mixed = jnp.einsum("hij,jhd->ihd", weights, values, preferred_element_type=jnp.float32)
        return mixed.astype(jnp.bfloat16)

    encoded = lax.map(attend, (query_groups, key_groups, value_group_list))
    encoded = encoded.transpose(1, 0, 2, 3).reshape(rows, width)
    starts = patch_starts[0, 0]
    nexts = jnp.concatenate([starts[1:], jnp.full((1,), rows, jnp.int32)])
    place = jnp.arange(rows, dtype=jnp.int32)[None, :]
    member = (place >= starts[:, None]) & (place < nexts[:, None])
    length = jnp.sum(member.astype(jnp.float32), axis=-1)
    summed = jnp.dot(member.astype(jnp.bfloat16), encoded, preferred_element_type=jnp.float32)
    pooled = (summed / jnp.maximum(length, 1.0)[:, None]).astype(jnp.bfloat16)
    valid = starts < rows

    patches = lax.all_gather(pooled, "z", axis=0, tiled=True)
    patches = lax.all_gather(patches, "c", axis=0, tiled=True)
    hidden_in = jnp.dot(patches, proj_cols, preferred_element_type=jnp.float32)
    activation = jax.nn.silu(hidden_in).astype(jnp.bfloat16)
    latent_part = jnp.einsum(
        "pk,dkj->pdj", activation, latent_w, preferred_element_type=jnp.float32
    ).astype(jnp.bfloat16)
    latent_part = latent_part.reshape(latent_part.shape[0], -1)
    latent = lax.psum_scatter(latent_part, "c", scatter_dimension=0, tiled=True)
    latent = lax.psum_scatter(latent, "z", scatter_dimension=0, tiled=True)

    cot_all = cot_all.reshape(cot_all.shape[0], ndp, lat_cols)
    back = jnp.einsum("pdj,dkj->pk", cot_all, latent_w, preferred_element_type=jnp.float32)
    sigma = jax.nn.sigmoid(hidden_in)
    act_grad = (back * sigma * (1.0 + hidden_in * (1.0 - sigma))).astype(jnp.bfloat16)
    gpart = lax.dot_general(
        act_grad, proj_cols, (((1,), (1,)), ((), ())), preferred_element_type=jnp.float32
    ).astype(jnp.bfloat16)
    grads = lax.psum_scatter(gpart, "c", scatter_dimension=0, tiled=True)
    grads = lax.psum_scatter(grads, "z", scatter_dimension=0, tiled=True).astype(jnp.float32)
    grads = jnp.where(valid[:, None], grads, 0.0)
    return (latent[None], grads.astype(jnp.bfloat16)[None])


def solution(mesh):
    n_dp = mesh.shape["dp"]
    n_bytes = mesh.shape["bytes"]
    side = int(round(math.sqrt(n_dp)))
    view = Mesh(
        np.asarray(mesh.devices).reshape(n_dp // side, side, n_bytes // 2, 2),
        DP_AXES + BYTE_AXES,
    )
    act = P(DP_AXES, BYTE_AXES, None)
    return jax.shard_map(
        per_device,
        mesh=view,
        in_specs=(act, act, act, act, P(DP_AXES, BYTE_AXES), P(BYTE_AXES, DP_AXES), act),
        out_specs=(act, act),
        check_vma=False,
    )
```

time: 236 us -> 245 us (1.038)
  the two profiles are of different devices: /device:TPU:131 before, /device:TPU:2 now
where the time goes in v1:
time: 245 us; the launch traced here: 244 us
  blocking collectives  119 us (49%)
  waiting for transfers between devices  41.2 us (17%)
  local copies, waits for them, and re-layouts  26.8 us (11%)
  starting transfers between devices  22.8 us (9%)
  matrix products  17.6 us (7%)
  between operations  14.8 us (6%)
    all_gather x1, blocking collectives, per_device(): cot = lax.all_gather(latent_cotangent[0], 'z', axis=0, tiled=True)  40.6 us
    unnamed x1, blocking collectives  26.1 us
    reduce_scatter x1, waiting for transfers between devices, per_device(): latent = lax.psum_scatter(latent_part, 'c', scatter_dimension=0, tiled=True)  25.4 us
    all_gather x1, blocking collectives, per_device(): wbuf = lax.all_gather(wbuf, 'x', axis=0)  25.1 us
    all_gather x1, blocking collectives, per_device(): patches = lax.all_gather(pooled, 'z', axis=0, tiled=True)  25 us
    unnamed x4, starting transfers between devices  12.5 us
    reduce_scatter x1, waiting for transfers between devices, per_device(): grads = lax.psum_scatter(gpart, 'c', scatter_dimension=0, tiled=True)  10.6 us
    ppermute x4, starting transfers between devices, shifted(): return lax.ppermute(shard, axis, pairs)  10.1 us
  transfers between devices with their start and end apart: 12, of which 4 were waited for; matrix products, arithmetic and copies ran while one was open for 11% of the time, Pallas kernels for 0%

profile of v1, /device:TPU:2, one launch (start us, length us, event | category | flops | bytes accessed | tf_op | source)
XLA Modules:
  0.0 244.1 jit_solution(2053453238898949843)
XLA Ops:
  8.3 40.6 %all-gather.2 = bf16[1,96,4096]{2,0,1:T(2,128)(2,1)S(1)} all-gather(bf16[1,12,4096]{2,0,1:T(2,128)(2,1)S(1)} %copy.52), channel_id=4, replica_groups=mesh['y'=8,'x'=8,'z'=8,'c'=2] {'z'}, dimensions={1}, use_global_device_ids=true | all-gather | bytes 884736 | tf_op jit(solution)/shard_map/all_gather | solution.py:40
  49.0 1.7 copy.53
  50.8 3.8 %collective-permute-start = (bf16[1,128,1024]{2,1,0:T(8,128)(2,1)S(1)}, bf16[1,128,1024]{2,1,0:T(8,128)(2,1)S(1)}, u32[]{:S(2)}, u32[]{:S(2)}) collective-permute-start(bf16[1,128,1024]{2,1,0:T(8,128)(2,1)S(1)} %copy-done.1), channel_id=1, source_target_pairs={{0,2},{1,3},{2,4},{3,5},{4,6},{5,7},{6,8},{7,9},{8,10},{9,11},{10,... | collective-permute-start | bytes 786440 | tf_op jit(solution)/shard_map/ppermute | solution.py:18
  54.6 1.3 collective-permute-start.1
  55.9 2.5 %collective-permute-start.2 = (bf16[1,128,1024]{2,1,0:T(8,128)(2,1)S(1)}, bf16[1,128,1024]{2,1,0:T(8,128)(2,1)S(1)}, u32[]{:S(2)}, u32[]{:S(2)}) collective-permute-start(bf16[1,128,1024]{2,1,0:T(8,128)(2,1)S(1)} %copy-done.2), channel_id=1, source_target_pairs={{0,2},{1,3},{2,4},{3,5},{4,6},{5,7},{6,8},{7,9},{8,10},{9,11},{10,... | collective-permute-start | bytes 786440 | tf_op jit(solution)/shard_map/ppermute | solution.py:18
  58.4 2.5 %collective-permute-start.3 = (bf16[1,128,1024]{2,1,0:T(8,128)(2,1)S(1)}, bf16[1,128,1024]{2,1,0:T(8,128)(2,1)S(1)}, u32[]{:S(2)}, u32[]{:S(2)}) collective-permute-start(bf16[1,128,1024]{2,1,0:T(8,128)(2,1)S(1)} %copy-done.2), channel_id=1, source_target_pairs={{0,1},{1,2},{2,3},{3,4},{4,5},{5,6},{6,7},{7,8},{8,9},{9,10},{10,1... | collective-permute-start | bytes 786440 | tf_op jit(solution)/shard_map/ppermute | solution.py:18
  61.2 25.1 %all-gather = bf16[163840]{0:T(1024)(128)(2,1)S(1)} all-gather(bf16[20480]{0:T(1024)(128)(2,1)S(1)} %pad_maximum_fusion), channel_id=2, replica_groups=mesh['y'=8,'x'=8,'z'=8,'c'=2] {'x'}, dimensions={0}, use_global_device_ids=true | all-gather | bytes 368640 | tf_op jit(solution)/shard_map/all_gather | solution.py:33
  89.2 10.4 %while.11 = (s32[]{:T(128)}, bf16[4,128,4,64]{1,3,2,0:T(8,128)(2,1)}, bf16[4,384,4,64]{1,3,2,0:T(8,128)(2,1)S(1)}, bf16[4,128,4,64]{1,3,2,0:T(8,128)(2,1)S(1)}, ...) while((s32[]{:T(128)}, ...), condition=%wide.region_3.4_spmd.clone, body=%wide.region_0.3_spmd.clone.sunk | while | flops 77497600 | bytes 3301333 | solution.py:71
  90.2 1.7 fusion.86
  92.8 1.7 fusion.86
  95.4 1.7 fusion.86
  98.0 1.7 fusion.86
  99.6 1.1 fusion.35
  100.8 25.0 %all-gather.4 = bf16[8,12,1024]{2,1,0:T(8,128)(2,1)S(1)} all-gather(bf16[1,12,1024]{2,1,0:T(8,128)(2,1)S(1)} %fusion.35), channel_id=1, replica_groups=mesh['y'=8,'x'=8,'z'=8,'c'=2] {'z'}, dimensions={0}, use_global_device_ids=true | all-gather | bytes 221184 | tf_op jit(solution)/shard_map/all_gather | solution.py:82
  125.8 2.1 all_gather.25
  127.9 3.8 %copy.54 = bf16[1,192,4096]{1,2,0:T(8,128)(2,1)} copy(bf16[1,192,4096]{2,1,0:T(8,128)(2,1)} %all-gather.10.cloned.1.call-done) | data formatting | bytes 3145728 | tf_op jit(solution)/shard_map/all_gather | solution.py:41
  131.7 3.6 %all-gather.8.cloned.1.call-done = bf16[64,20480]{1,0:T(8,128)(2,1)} async-done(((bf16[8,20480]{1,0:T(8,128)(2,1)}), bf16[64,20480]{1,0:T(8,128)(2,1)}) %all-gather.8.cloned.1.call-update) | async-done | bytes 2621456 | tf_op jit(solution)/shard_map/all_gather | solution.py:34
  135.4 1.1 slice.16
  136.7 1.6 slice-done
  138.3 5.5 %reshape.85 = bf16[64,256,64]{2,1,0:T(8,128)(2,1)} reshape(bf16[64,16384]{1,0:T(8,128)(2,1)S(1)} %slice-done) | data formatting | bytes 4194304 | tf_op jit(solution)/shard_map/reshape | solution.py:38
  144.1 5.5 %convolution_convert_fusion.1 = bf16[192,1024]{1,0:T(8,128)(2,1)} fusion(bf16[1024,256]{1,0:T(8,128)(2,1)S(1)} %reshape.84, bf16[64,256,64]{2,1,0:T(8,128)(2,1)} %reshape.85, bf16[192,64,64]{0,2,1:T(8,128)(2,1)} %bitcast.101, f32[192,256]{1,0:T(8,128)S(1)} %fusion.58), kind=kOutput, calls=%fused_computation.28 | convolution fusion | flops 503955456 | bytes 4784128 | tf_op jit(solution)/shard_map/dot_general | solution.py:97
  149.6 3.5 %copy.50 = bf16[64,256,64]{1,2,0:T(8,128)(2,1)S(1)} copy(bf16[64,256,64]{2,1,0:T(8,128)(2,1)} %reshape.85) | data formatting | bytes 4194304 | tf_op jit(solution)/shard_map/reshape | solution.py:38
  154.2 2.8 %copy.51 = bf16[192,4096]{1,0:T(8,128)(2,1)} copy(bf16[192,4096]{0,1:T(8,128)(2,1)S(1)} %bitcast.100) | data formatting | bytes 3145728 | tf_op jit(solution)/shard_map/reshape | solution.py:89
  157.1 10.6 %reduce-scatter.9.cloned.1.call-done = bf16[96,1024]{1,0:T(8,128)(2,1)} async-done(((bf16[192,1024]{1,0:T(8,128)(2,1)}), bf16[96,1024]{1,0:T(8,128)(2,1)}) %reduce-scatter.9.cloned.1.call-update) | async-done | bytes 196624 | tf_op jit(solution)/shard_map/reduce_scatter | solution.py:100
  167.7 25.4 %reduce-scatter.7.cloned.1.call-done = bf16[96,4096]{1,0:T(8,128)(2,1)} async-done(((bf16[192,4096]{1,0:T(8,128)(2,1)}), bf16[96,4096]{1,0:T(8,128)(2,1)}) %reduce-scatter.7.cloned.1.call-update) | async-done | bytes 786448 | tf_op jit(solution)/shard_map/reduce_scatter | solution.py:90
  193.1 26.1 %fusion.52 = (bf16[16,4096]{1,0:T(8,128)(2,1)S(1)}, bf16[16,1024]{1,0:T(8,128)(2,1)S(1)}) fusion(bf16[96,4096]{1,0:T(8,128)(2,1)} %reduce-scatter.7.cloned.1.call-done, bf16[96,1024]{1,0:T(8,128)(2,1)} %reduce-scatter.9.cloned.1.call-done), kind=kCustom, calls=%all-reduce-scatter.2 | all-reduce-scatter fusion | flops 655361 | bytes 1150976
  219.3 2.3 collective-permute-start.6
  221.5 3.0 %collective-permute-start.7 = (bf16[12,1024]{1,0:T(8,128)(2,1)S(1)}, bf16[12,1024]{1,0:T(8,128)(2,1)S(1)}, u32[]{:S(2)}, u32[]{:S(2)}) collective-permute-start(bf16[12,1024]{1,0:T(8,128)(2,1)S(1)} %slice.19), channel_id=1, source_target_pairs={{0,4},{2,6},{4,8},{6,10},{8,12},{10,14},{1,5},{3,7},{5,9},{7,11},{... | collective-permute-start | bytes 73736
  224.5 1.3 dynamic-slice.6
  226.5 4.0 %collective-permute-start.4 = (bf16[16,4096]{1,0:T(8,128)(2,1)S(1)}, bf16[16,4096]{1,0:T(8,128)(2,1)S(1)}, u32[]{:S(2)}, u32[]{:S(2)}) collective-permute-start(bf16[16,4096]{1,0:T(8,128)(2,1)S(1)} %get-tuple-element.69), channel_id=1, source_target_pairs={{0,2},{2,4},{4,6},{6,8},{8,10},{10,12},{12,14},{1,3},{3,5},{5,7},{... | collective-permute-start | bytes 393224
  230.6 3.2 %collective-permute-start.5 = (bf16[12,4096]{1,0:T(8,128)(2,1)S(1)}, bf16[12,4096]{1,0:T(8,128)(2,1)S(1)}, u32[]{:S(2)}, u32[]{:S(2)}) collective-permute-start(bf16[12,4096]{1,0:T(8,128)(2,1)S(1)} %slice.18), channel_id=1, source_target_pairs={{0,4},{2,6},{4,8},{6,10},{8,12},{10,14},{1,5},{3,7},{5,9},{7,11},{... | collective-permute-start | bytes 294920
  234.8 1.5 collective-permute-done.5
  (74 shorter events, 11.9 us)
Async XLA Ops:
  7.2 120.7 %all-gather.10.cloned.1.call-start = ((), (), s32[]{:S(2)}) async-start(), calls=%async_computation.5 | async-start | bytes 2359296 | tf_op jit(solution)/shard_map/all_gather | solution.py:41
  8.3 42.5 %copy-start.1 = (bf16[1,128,1024]{2,1,0:T(8,128)(2,1)S(1)}, bf16[1,128,1024]{2,1,0:T(8,128)(2,1)}, u32[]{:S(2)}) copy-start(bf16[1,128,1024]{2,1,0:T(8,128)(2,1)} %param.11) | copy-start | bytes 786436
  8.3 47.6 %copy-start.2 = (bf16[1,128,1024]{2,1,0:T(8,128)(2,1)S(1)}, bf16[1,128,1024]{2,1,0:T(8,128)(2,1)}, u32[]{:S(2)}) copy-start(bf16[1,128,1024]{2,1,0:T(8,128)(2,1)} %param.10) | copy-start | bytes 786436
  8.3 52.7 %copy-start.3 = (bf16[256,64]{0,1:T(8,128)(2,1)S(1)}, bf16[256,64]{0,1:T(8,128)(2,1)}, u32[]{:S(2)}) copy-start(bf16[256,64]{0,1:T(8,128)(2,1)} %param.14) | copy-start | bytes 98308
  49.0 12.2 %copy-start.4 = (bf16[16,256]{1,0:T(8,128)(2,1)S(1)}, bf16[16,256]{1,0:T(8,128)(2,1)}, u32[]{:S(2)}) copy-start(bf16[16,256]{1,0:T(8,128)(2,1)} %param.13) | copy-start | bytes 24580
  49.0 38.3 %copy-start.5 = (s32[1,1,12]{2,1,0:T(1,128)S(1)}, s32[1,1,12]{2,1,0:T(1,128)}, u32[]{:S(2)}) copy-start(s32[1,1,12]{2,1,0:T(1,128)} %param.12) | copy-start | bytes 148
  50.7 37.3 %copy-start = (bf16[1,128,1024]{2,1,0:T(8,128)(2,1)S(1)}, bf16[1,128,1024]{2,1,0:T(8,128)(2,1)}, u32[]{:S(2)}) copy-start(bf16[1,128,1024]{2,1,0:T(8,128)(2,1)} %param.9) | copy-start | bytes 786436
  50.7 84.6 %all-gather.8.cloned.1.call-start = ((), (), s32[]{:S(2)}) async-start(), calls=%async_computation.4 | async-start | bytes 2949120 | tf_op jit(solution)/shard_map/all_gather | solution.py:34
  50.8 37.4 %collective-permute-start = (bf16[1,128,1024]{2,1,0:T(8,128)(2,1)S(1)}, bf16[1,128,1024]{2,1,0:T(8,128)(2,1)S(1)}, u32[]{:S(2)}, u32[]{:S(2)}) collective-permute-start(bf16[1,128,1024]{2,1,0:T(8,128)(2,1)S(1)} %copy-done.1), channel_id=1, source_target_pairs={{0,2},{1,3},{2,4},{3,5},{4,6},{5,7},{6,8},{7,9},{8,10},{9,11},{10,... | collective-permute-start | bytes 786440 | tf_op jit(solution)/shard_map/ppermute | solution.py:18
  54.6 33.8 %collective-permute-start.1 = (bf16[1,128,1024]{2,1,0:T(8,128)(2,1)S(1)}, bf16[1,128,1024]{2,1,0:T(8,128)(2,1)S(1)}, u32[]{:S(2)}, u32[]{:S(2)}) collective-permute-start(bf16[1,128,1024]{2,1,0:T(8,128)(2,1)S(1)} %copy-done.1), channel_id=1, source_target_pairs={{0,1},{1,2},{2,3},{3,4},{4,5},{5,6},{6,7},{7,8},{8,9},{9,10},{10,1... | collective-permute-start | bytes 786440 | tf_op jit(solution)/shard_map/ppermute | solution.py:18
  55.9 32.7 %collective-permute-start.2 = (bf16[1,128,1024]{2,1,0:T(8,128)(2,1)S(1)}, bf16[1,128,1024]{2,1,0:T(8,128)(2,1)S(1)}, u32[]{:S(2)}, u32[]{:S(2)}) collective-permute-start(bf16[1,128,1024]{2,1,0:T(8,128)(2,1)S(1)} %copy-done.2), channel_id=1, source_target_pairs={{0,2},{1,3},{2,4},{3,5},{4,6},{5,7},{6,8},{7,9},{8,10},{9,11},{10,... | collective-permute-start | bytes 786440 | tf_op jit(solution)/shard_map/ppermute | solution.py:18
  58.4 30.3 %collective-permute-start.3 = (bf16[1,128,1024]{2,1,0:T(8,128)(2,1)S(1)}, bf16[1,128,1024]{2,1,0:T(8,128)(2,1)S(1)}, u32[]{:S(2)}, u32[]{:S(2)}) collective-permute-start(bf16[1,128,1024]{2,1,0:T(8,128)(2,1)S(1)} %copy-done.2), channel_id=1, source_target_pairs={{0,1},{1,2},{2,3},{3,4},{4,5},{5,6},{6,7},{7,8},{8,9},{9,10},{10,1... | collective-permute-start | bytes 786440 | tf_op jit(solution)/shard_map/ppermute | solution.py:18
  87.2 80.5 %reduce-scatter.9.cloned.1.call-start = ((), (), s32[]{:S(2)}) async-start(), calls=%async_computation.3 | async-start | bytes 589824 | tf_op jit(solution)/shard_map/reduce_scatter | solution.py:100
  136.7 1.6 slice-start
  149.6 43.5 %reduce-scatter.7.cloned.1.call-start = ((), (), s32[]{:S(2)}) async-start(), calls=%async_computation.2 | async-start | bytes 2359296 | tf_op jit(solution)/shard_map/reduce_scatter | solution.py:90
  219.3 14.5 %collective-permute-start.6 = (bf16[16,1024]{1,0:T(8,128)(2,1)S(1)}, bf16[16,1024]{1,0:T(8,128)(2,1)S(1)}, u32[]{:S(2)}, u32[]{:S(2)}) collective-permute-start(bf16[16,1024]{1,0:T(8,128)(2,1)S(1)} %get-tuple-element.70), channel_id=1, source_target_pairs={{0,2},{2,4},{4,6},{6,8},{8,10},{10,12},{12,14},{1,3},{3,5},{5,7},{... | collective-permute-start | bytes 98312
  221.5 12.2 %collective-permute-start.7 = (bf16[12,1024]{1,0:T(8,128)(2,1)S(1)}, bf16[12,1024]{1,0:T(8,128)(2,1)S(1)}, u32[]{:S(2)}, u32[]{:S(2)}) collective-permute-start(bf16[12,1024]{1,0:T(8,128)(2,1)S(1)} %slice.19), channel_id=1, source_target_pairs={{0,4},{2,6},{4,8},{6,10},{8,12},{10,14},{1,5},{3,7},{5,9},{7,11},{... | collective-permute-start | bytes 73736
  226.5 9.7 %collective-permute-start.4 = (bf16[16,4096]{1,0:T(8,128)(2,1)S(1)}, bf16[16,4096]{1,0:T(8,128)(2,1)S(1)}, u32[]{:S(2)}, u32[]{:S(2)}) collective-permute-start(bf16[16,4096]{1,0:T(8,128)(2,1)S(1)} %get-tuple-element.69), channel_id=1, source_target_pairs={{0,2},{2,4},{4,6},{6,8},{8,10},{10,12},{12,14},{1,3},{3,5},{5,7},{... | collective-permute-start | bytes 393224
  230.6 5.7 %collective-permute-start.5 = (bf16[12,4096]{1,0:T(8,128)(2,1)S(1)}, bf16[12,4096]{1,0:T(8,128)(2,1)S(1)}, u32[]{:S(2)}, u32[]{:S(2)}) collective-permute-start(bf16[12,4096]{1,0:T(8,128)(2,1)S(1)} %slice.18), channel_id=1, source_target_pairs={{0,4},{2,6},{4,8},{6,10},{8,12},{10,14},{1,5},{3,7},{5,9},{7,11},{... | collective-permute-start | bytes 294920
Sparse Core Ops, SparseCore 0:
  50.9 19.4 all-gather.9
  87.3 47.9 all-gather.7
  149.7 17.9 reduce-scatter.8
  171.3 21.7 reduce-scatter.6

commit v2 on v0

--- a/solution.py
+++ b/solution.py
@@ -3,9 +3,13 @@
 import jax
 import jax.numpy as jnp
 from jax import lax
+import numpy as np
+from jax.sharding import Mesh
 from jax.sharding import PartitionSpec as P
 
 HEAD_L = 64
+BYTE_AXES = ("z", "c")
+DP_AXES = ("y", "x")
 
 
 def shifted(shard, axis, by):
@@ -24,7 +28,7 @@
     groups = heads // group_size
     received = {}
     for reach in (2, 1):
-        received[reach] = shifted((byte_keys, byte_values), "bytes", reach)
+        received[reach] = shifted((byte_keys, byte_values), BYTE_AXES, reach)
     keys_all = jnp.concatenate([received[2][0][0], received[1][0][0], byte_keys[0]], axis=0)
     values_all = jnp.concatenate([received[2][1][0], received[1][1][0], byte_values[0]], axis=0)
     query_groups = byte_queries[0].reshape(rows, groups, group_size, HEAD_L).transpose(1, 0, 2, 3)
@@ -34,7 +38,7 @@
     )
     qpos = jnp.arange(rows, dtype=jnp.int32)[:, None] + 2 * rows
     kpos = jnp.arange(3 * rows, dtype=jnp.int32)[None, :]
-    position = lax.axis_index("bytes")
+    position = lax.axis_index(BYTE_AXES)
     reachable = (kpos >= 2 * rows) | (kpos >= rows) & (position >= 1) | (position >= 2)
     allowed = (kpos <= qpos) & (kpos > qpos - 2 * rows) & reachable
 
@@ -60,21 +64,26 @@
     summed = jnp.dot(member.astype(jnp.bfloat16), encoded, preferred_element_type=jnp.float32)
     pooled = (summed / jnp.maximum(length, 1.0)[:, None]).astype(jnp.bfloat16)
     valid = starts < rows
-    proj_cols, latent_row_list = (
-        lax.all_gather(patch_proj, "dp", axis=0, tiled=True),
-        lax.all_gather(latent_proj, "dp", axis=1, tiled=True),
-    )
-    patches = lax.all_gather(pooled[None], "bytes", axis=1, tiled=True)
+    pr, bl = patch_proj.shape
+    lr, lc = latent_proj.shape
+    wbuf = jnp.concatenate([patch_proj.reshape(-1), latent_proj.reshape(-1)])
+    wbuf = lax.all_gather(wbuf, "x", axis=0)
+    wbuf = lax.all_gather(wbuf, "y", axis=0)
+    ndp = wbuf.shape[0] * wbuf.shape[1]
+    wbuf = wbuf.reshape(ndp, -1)
+    proj_cols = wbuf[:, : pr * bl].reshape(ndp * pr, bl)
+    latent_row_list = wbuf[:, pr * bl :].reshape(ndp, lr, lc).transpose(1, 0, 2).reshape(lr, ndp * lc)
+    patches = lax.all_gather(pooled[None], BYTE_AXES, axis=1, tiled=True)
     hidden_in = jnp.dot(patches[0], proj_cols, preferred_element_type=jnp.float32)
     activation = jax.nn.silu(hidden_in).astype(jnp.bfloat16)
     piece = activation
     latent = lax.psum_scatter(
         jnp.dot(piece, latent_row_list, preferred_element_type=jnp.float32).astype(jnp.bfloat16),
-        "bytes",
+        BYTE_AXES,
         scatter_dimension=0,
         tiled=True,
     )
-    cot_all = lax.all_gather(latent_cotangent, "bytes", axis=1, tiled=True)
+    cot_all = lax.all_gather(latent_cotangent, BYTE_AXES, axis=1, tiled=True)
     back = lax.dot_general(
         cot_all[0], latent_row_list, (((1,), (1,)), ((), ())), preferred_element_type=jnp.float32
     )
@@ -85,7 +94,7 @@
         lax.dot_general(
             piece, proj_cols, (((1,), (1,)), ((), ())), preferred_element_type=jnp.float32
         ).astype(jnp.bfloat16),
-        "bytes",
+        BYTE_AXES,
         scatter_dimension=0,
         tiled=True,
     ).astype(jnp.float32)
@@ -94,18 +103,18 @@
 
 
 def solution(mesh):
+    n_dp = mesh.shape["dp"]
+    n_bytes = mesh.shape["bytes"]
+    side = int(round(math.sqrt(n_dp)))
+    view = Mesh(
+        np.asarray(mesh.devices).reshape(n_dp // side, side, n_bytes // 2, 2),
+        DP_AXES + BYTE_AXES,
+    )
+    act = P(DP_AXES, BYTE_AXES, None)
     return jax.shard_map(
         per_device,
-        mesh=mesh,
-        in_specs=(
-            P("dp", "bytes", None),
-            P("dp", "bytes", None),
-            P("dp", "bytes", None),
-            P("dp", "bytes", None),
-            P("dp", "bytes"),
-            P("bytes", "dp"),
-            P("dp", "bytes", None),
-        ),
-        out_specs=(P("dp", "bytes", None), P("dp", "bytes", None)),
+        mesh=view,
+        in_specs=(act, act, act, act, P(DP_AXES, BYTE_AXES), P(BYTE_AXES, DP_AXES), act),
+        out_specs=(act, act),
         check_vma=False,
     )

time: 236 us -> 219 us (0.928)
  the two profiles are of different devices: /device:TPU:131 before, /device:TPU:129 now
where the time goes in v2:
time: 219 us; the launch traced here: 218 us
  blocking collectives  71.5 us (33%)
  starting transfers between devices  50.9 us (23%)
  waiting for transfers between devices  39.8 us (18%)
  local copies, waits for them, and re-layouts  21.5 us (10%)
  matrix products  17.5 us (8%)
  between operations  15.1 us (7%)
    all_gather x1, waiting for transfers between devices, per_device(): cot_all = lax.all_gather(latent_cotangent, BYTE_AXES, axis=1, tiled=True)  32.4 us
    unnamed x1, blocking collectives  27.5 us
    unnamed x8, starting transfers between devices  25.8 us
    ppermute x4, starting transfers between devices, shifted(): return lax.ppermute(shard, axis, pairs)  25 us
    all_gather x1, blocking collectives, per_device(): patches = lax.all_gather(pooled[None], BYTE_AXES, axis=1, tiled=True)  24 us
    all_gather x1, blocking collectives, per_device(): wbuf = lax.all_gather(wbuf, 'x', axis=0)  20 us
    unnamed x20, local copies, waits for them, and re-layouts  7.15 us
    dot_general x4, matrix products, attend(): jnp.einsum('hij,jhd->ihd', weights, values, preferred_element_type=jnp.fl...  6.69 us
  transfers between devices with their start and end apart: 14, of which 3 were waited for; matrix products, arithmetic and copies ran while one was open for 14% of the time, Pallas kernels for 0%

profile of v2, /device:TPU:129, one launch (start us, length us, event | category | flops | bytes accessed | tf_op | source)
XLA Modules:
  0.0 218.1 jit_solution(811689937012413546)
XLA Ops:
  9.0 20.0 %all-gather.1 = bf16[163840]{0:T(1024)(128)(2,1)S(1)} all-gather(bf16[20480]{0:T(1024)(128)(2,1)S(1)} %pad_maximum_fusion), channel_id=3, replica_groups=mesh['y'=8,'x'=8,'z'=8,'c'=2] {'x'}, dimensions={0}, use_global_device_ids=true | all-gather | bytes 368640 | tf_op jit(solution)/shard_map/all_gather | solution.py:70
  29.9 4.9 %collective-permute-start = (bf16[1,128,1024]{2,1,0:T(8,128)(2,1)}, bf16[1,128,1024]{2,1,0:T(8,128)(2,1)S(1)}, u32[]{:S(2)}, u32[]{:S(2)}) collective-permute-start(bf16[1,128,1024]{2,1,0:T(8,128)(2,1)} %param.11), channel_id=1, source_target_pairs={{0,2},{1,3},{2,4},{3,5},{4,6},{5,7},{6,8},{7,9},{8,10},{9,11},{10,... | collective-permute-start | bytes 786440 | tf_op jit(solution)/shard_map/ppermute | solution.py:18
  34.8 11.8 %collective-permute-start.1 = (bf16[1,128,1024]{2,1,0:T(8,128)(2,1)}, bf16[1,128,1024]{2,1,0:T(8,128)(2,1)S(1)}, u32[]{:S(2)}, u32[]{:S(2)}) collective-permute-start(bf16[1,128,1024]{2,1,0:T(8,128)(2,1)} %param.11), channel_id=1, source_target_pairs={{0,1},{1,2},{2,3},{3,4},{4,5},{5,6},{6,7},{7,8},{8,9},{9,10},{10,1... | collective-permute-start | bytes 786440 | tf_op jit(solution)/shard_map/ppermute | solution.py:18
  46.6 6.1 %collective-permute-start.2 = (bf16[1,128,1024]{2,1,0:T(8,128)(2,1)}, bf16[1,128,1024]{2,1,0:T(8,128)(2,1)S(1)}, u32[]{:S(2)}, u32[]{:S(2)}) collective-permute-start(bf16[1,128,1024]{2,1,0:T(8,128)(2,1)} %param.10), channel_id=1, source_target_pairs={{0,2},{1,3},{2,4},{3,5},{4,6},{5,7},{6,8},{7,9},{8,10},{9,11},{10,... | collective-permute-start | bytes 786440 | tf_op jit(solution)/shard_map/ppermute | solution.py:18
  52.8 2.2 %collective-permute-start.3 = (bf16[1,128,1024]{2,1,0:T(8,128)(2,1)}, bf16[1,128,1024]{2,1,0:T(8,128)(2,1)S(1)}, u32[]{:S(2)}, u32[]{:S(2)}) collective-permute-start(bf16[1,128,1024]{2,1,0:T(8,128)(2,1)} %param.10), channel_id=1, source_target_pairs={{0,1},{1,2},{2,3},{3,4},{4,5},{5,6},{6,7},{7,8},{8,9},{9,10},{10,1... | collective-permute-start | bytes 786440 | tf_op jit(solution)/shard_map/ppermute | solution.py:18
  55.0 1.8 copy.54
  59.6 10.5 %while.11 = (s32[]{:T(128)}, bf16[4,128,4,64]{1,3,2,0:T(8,128)(2,1)}, bf16[4,384,4,64]{1,3,2,0:T(8,128)(2,1)S(1)}, bf16[4,128,4,64]{1,3,2,0:T(8,128)(2,1)S(1)}, ...) while((s32[]{:T(128)}, ...), condition=%wide.region_3.4_spmd.clone, body=%wide.region_0.3_spmd.clone.sunk | while | flops 77497600 | bytes 3301333 | solution.py:57
  60.5 1.7 fusion.98
  63.2 1.7 fusion.98
  65.8 1.7 fusion.98
  68.4 1.7 fusion.98
  70.1 1.1 fusion.49
  71.2 24.0 %all-gather.3 = bf16[16,12,1024]{2,1,0:T(8,128)(2,1)S(1)} all-gather(bf16[1,12,1024]{2,1,0:T(8,128)(2,1)S(1)} %fusion.49), channel_id=2, replica_groups=mesh['y'=8,'x'=8,'z'=8,'c'=2] {'z','c'}, dimensions={0}, use_global_device_ids=true | all-gather | bytes 417792 | tf_op jit(solution)/shard_map/all_gather | solution.py:76
  95.4 1.1 slice.16
  96.7 1.6 slice-done
  98.3 5.5 %reshape.82 = bf16[64,256,64]{2,1,0:T(8,128)(2,1)} reshape(bf16[64,16384]{1,0:T(8,128)(2,1)S(1)} %slice-done) | data formatting | bytes 4194304 | tf_op jit(solution)/shard_map/reshape | solution.py:75
  103.8 3.5 %copy.53 = bf16[256,64,64]{0,2,1:T(8,128)(2,1)S(1)} copy(bf16[256,64,64]{2,0,1:T(8,128)(2,1)} %bitcast.104) | data formatting | bytes 4194304 | tf_op jit(solution)/shard_map/transpose | solution.py:75
  107.6 2.0 convolution_convert_fusion.1
  109.6 32.4 %all-gather.7.cloned.1.call-done = bf16[1,192,4096]{2,0,1:T(2,128)(2,1)} async-done(((bf16[1,12,4096]{2,0,1:T(2,128)(2,1)}), bf16[1,192,4096]{2,0,1:T(2,128)(2,1)}) %all-gather.7.cloned.1.call-update) | async-done | bytes 1572880 | tf_op jit(solution)/shard_map/all_gather | solution.py:86
  142.1 4.1 %convolution_convert_fusion.2 = bf16[192,1024]{1,0:T(8,128)(2,1)S(1)} fusion(bf16[1024,256]{1,0:T(8,128)(2,1)S(1)} %reshape.81, bf16[256,4096]{0,1:T(8,128)(2,1)S(1)} %bitcast.106, bf16[1,192,4096]{2,0,1:T(2,128)(2,1)} %all-gather.7.cloned.1.call-done, f32[192,256]{1,0:T(8,128)S(1)} %fusion.71), kind=kOutput, calls=%fused_computation.32 | convolution fusion | flops 503955456 | bytes 4784128 | tf_op jit(solution)/shard_map/dot_general | solution.py:94
  146.1 27.5 %fusion.65 = (bf16[16,4096]{1,0:T(8,128)(2,1)S(1)}, bf16[16,1024]{1,0:T(8,128)(2,1)S(1)}) fusion(bf16[192,4096]{1,0:T(8,128)(2,1)} %convolution_convert_fusion.1, bf16[192,1024]{1,0:T(8,128)(2,1)S(1)} %convolution_convert_fusion.2), kind=kCustom, calls=%all-reduce-scatter.2 | all-reduce-scatter fusion | flops 1310721 | bytes 2134016
  173.7 5.7 %collective-permute-start.10 = (bf16[16,1024]{1,0:T(8,128)(2,1)S(1)}, bf16[16,1024]{1,0:T(8,128)(2,1)S(1)}, u32[]{:S(2)}, u32[]{:S(2)}) collective-permute-start(bf16[16,1024]{1,0:T(8,128)(2,1)S(1)} %get-tuple-element.70), channel_id=1, source_target_pairs={{0,3},{1,4},{2,5},{3,6},{4,7},{5,8},{6,9},{7,10},{8,11},{9,12},{10... | collective-permute-start | bytes 98312
  179.4 3.6 %collective-permute-start.8 = (bf16[16,1024]{1,0:T(8,128)(2,1)S(1)}, bf16[16,1024]{1,0:T(8,128)(2,1)S(1)}, u32[]{:S(2)}, u32[]{:S(2)}) collective-permute-start(bf16[16,1024]{1,0:T(8,128)(2,1)S(1)} %get-tuple-element.70), channel_id=1, source_target_pairs={{0,1},{1,2},{2,3},{3,4},{4,5},{5,6},{6,7},{7,8},{8,9},{9,10},{10,1... | collective-permute-start | bytes 98312
  182.9 4.9 %collective-permute-start.9 = (bf16[16,1024]{1,0:T(8,128)(2,1)S(1)}, bf16[16,1024]{1,0:T(8,128)(2,1)S(1)}, u32[]{:S(2)}, u32[]{:S(2)}) collective-permute-start(bf16[16,1024]{1,0:T(8,128)(2,1)S(1)} %get-tuple-element.70), channel_id=1, source_target_pairs={{0,2},{1,3},{2,4},{3,5},{4,6},{5,7},{6,8},{7,9},{8,10},{9,11},{10,... | collective-permute-start | bytes 98312
  187.9 1.9 collective-permute-start.11
  189.8 1.3 dynamic-slice.6
  191.8 2.3 %collective-permute-start.4 = (bf16[16,4096]{1,0:T(8,128)(2,1)S(1)}, bf16[16,4096]{1,0:T(8,128)(2,1)S(1)}, u32[]{:S(2)}, u32[]{:S(2)}) collective-permute-start(bf16[16,4096]{1,0:T(8,128)(2,1)S(1)} %get-tuple-element.69), channel_id=1, source_target_pairs={{0,1},{1,2},{2,3},{3,4},{4,5},{5,6},{6,7},{7,8},{8,9},{9,10},{10,1... | collective-permute-start | bytes 393224
  194.1 2.1 collective-permute-start.5
  196.2 3.8 %collective-permute-start.6 = (bf16[16,4096]{1,0:T(8,128)(2,1)S(1)}, bf16[16,4096]{1,0:T(8,128)(2,1)S(1)}, u32[]{:S(2)}, u32[]{:S(2)}) collective-permute-start(bf16[16,4096]{1,0:T(8,128)(2,1)S(1)} %get-tuple-element.69), channel_id=1, source_target_pairs={{0,3},{1,4},{2,5},{3,6},{4,7},{5,8},{6,9},{7,10},{8,11},{9,12},{10... | collective-permute-start | bytes 393224
  200.1 1.5 collective-permute-start.7
  202.9 6.4 %collective-permute-done.7 = bf16[12,4096]{1,0:T(8,128)(2,1)S(1)} collective-permute-done((bf16[12,4096]{1,0:T(8,128)(2,1)S(1)}, bf16[12,4096]{1,0:T(8,128)(2,1)S(1)}, u32[]{:S(2)}, u32[]{:S(2)}) %collective-permute-start.7) | collective-permute-done | bytes 98336
  209.4 1.2 concatenate.36
  (66 shorter events, 11.8 us)
Async XLA Ops:
  7.2 50.2 %copy-start.1 = (bf16[1,128,1024]{2,1,0:T(8,128)(2,1)S(1)}, bf16[1,128,1024]{2,1,0:T(8,128)(2,1)}, u32[]{:S(2)}) copy-start(bf16[1,128,1024]{2,1,0:T(8,128)(2,1)} %param.11) | copy-start | bytes 786436
  7.2 50.0 %copy-start.2 = (bf16[1,128,1024]{2,1,0:T(8,128)(2,1)S(1)}, bf16[1,128,1024]{2,1,0:T(8,128)(2,1)}, u32[]{:S(2)}) copy-start(bf16[1,128,1024]{2,1,0:T(8,128)(2,1)} %param.10) | copy-start | bytes 786436
  7.2 49.6 %copy-start.3 = (s32[1,1,12]{2,1,0:T(1,128)S(1)}, s32[1,1,12]{2,1,0:T(1,128)}, u32[]{:S(2)}) copy-start(s32[1,1,12]{2,1,0:T(1,128)} %param.12) | copy-start | bytes 148
  7.2 50.3 %copy-start = (bf16[1,128,1024]{2,1,0:T(8,128)(2,1)S(1)}, bf16[1,128,1024]{2,1,0:T(8,128)(2,1)}, u32[]{:S(2)}) copy-start(bf16[1,128,1024]{2,1,0:T(8,128)(2,1)} %param.9) | copy-start | bytes 786436
  7.2 88.1 %all-gather.9.cloned.1.call-start = ((), (), s32[]{:S(2)}) async-start(), calls=%async_computation.1 | async-start | bytes 2949120 | tf_op jit(solution)/shard_map/all_gather | solution.py:71
  29.9 112.2 %all-gather.7.cloned.1.call-start = ((), (), s32[]{:S(2)}) async-start(), calls=%async_computation | async-start | bytes 3342336 | tf_op jit(solution)/shard_map/all_gather | solution.py:86
  29.9 27.8 %collective-permute-start = (bf16[1,128,1024]{2,1,0:T(8,128)(2,1)}, bf16[1,128,1024]{2,1,0:T(8,128)(2,1)S(1)}, u32[]{:S(2)}, u32[]{:S(2)}) collective-permute-start(bf16[1,128,1024]{2,1,0:T(8,128)(2,1)} %param.11), channel_id=1, source_target_pairs={{0,2},{1,3},{2,4},{3,5},{4,6},{5,7},{6,8},{7,9},{8,10},{9,11},{10,... | collective-permute-start | bytes 786440 | tf_op jit(solution)/shard_map/ppermute | solution.py:18
  34.8 23.0 %collective-permute-start.1 = (bf16[1,128,1024]{2,1,0:T(8,128)(2,1)}, bf16[1,128,1024]{2,1,0:T(8,128)(2,1)S(1)}, u32[]{:S(2)}, u32[]{:S(2)}) collective-permute-start(bf16[1,128,1024]{2,1,0:T(8,128)(2,1)} %param.11), channel_id=1, source_target_pairs={{0,1},{1,2},{2,3},{3,4},{4,5},{5,6},{6,7},{7,8},{8,9},{9,10},{10,1... | collective-permute-start | bytes 786440 | tf_op jit(solution)/shard_map/ppermute | solution.py:18
  46.6 11.4 %collective-permute-start.2 = (bf16[1,128,1024]{2,1,0:T(8,128)(2,1)}, bf16[1,128,1024]{2,1,0:T(8,128)(2,1)S(1)}, u32[]{:S(2)}, u32[]{:S(2)}) collective-permute-start(bf16[1,128,1024]{2,1,0:T(8,128)(2,1)} %param.10), channel_id=1, source_target_pairs={{0,2},{1,3},{2,4},{3,5},{4,6},{5,7},{6,8},{7,9},{8,10},{9,11},{10,... | collective-permute-start | bytes 786440 | tf_op jit(solution)/shard_map/ppermute | solution.py:18
  52.8 6.4 %collective-permute-start.3 = (bf16[1,128,1024]{2,1,0:T(8,128)(2,1)}, bf16[1,128,1024]{2,1,0:T(8,128)(2,1)S(1)}, u32[]{:S(2)}, u32[]{:S(2)}) collective-permute-start(bf16[1,128,1024]{2,1,0:T(8,128)(2,1)} %param.10), channel_id=1, source_target_pairs={{0,1},{1,2},{2,3},{3,4},{4,5},{5,6},{6,7},{7,8},{8,9},{9,10},{10,1... | collective-permute-start | bytes 786440 | tf_op jit(solution)/shard_map/ppermute | solution.py:18
  96.7 1.6 slice-start
  173.7 22.5 %collective-permute-start.10 = (bf16[16,1024]{1,0:T(8,128)(2,1)S(1)}, bf16[16,1024]{1,0:T(8,128)(2,1)S(1)}, u32[]{:S(2)}, u32[]{:S(2)}) collective-permute-start(bf16[16,1024]{1,0:T(8,128)(2,1)S(1)} %get-tuple-element.70), channel_id=1, source_target_pairs={{0,3},{1,4},{2,5},{3,6},{4,7},{5,8},{6,9},{7,10},{8,11},{9,12},{10... | collective-permute-start | bytes 98312
  179.4 20.7 %collective-permute-start.8 = (bf16[16,1024]{1,0:T(8,128)(2,1)S(1)}, bf16[16,1024]{1,0:T(8,128)(2,1)S(1)}, u32[]{:S(2)}, u32[]{:S(2)}) collective-permute-start(bf16[16,1024]{1,0:T(8,128)(2,1)S(1)} %get-tuple-element.70), channel_id=1, source_target_pairs={{0,1},{1,2},{2,3},{3,4},{4,5},{5,6},{6,7},{7,8},{8,9},{9,10},{10,1... | collective-permute-start | bytes 98312
  182.9 18.7 %collective-permute-start.9 = (bf16[16,1024]{1,0:T(8,128)(2,1)S(1)}, bf16[16,1024]{1,0:T(8,128)(2,1)S(1)}, u32[]{:S(2)}, u32[]{:S(2)}) collective-permute-start(bf16[16,1024]{1,0:T(8,128)(2,1)S(1)} %get-tuple-element.70), channel_id=1, source_target_pairs={{0,2},{1,3},{2,4},{3,5},{4,6},{5,7},{6,8},{7,9},{8,10},{9,11},{10,... | collective-permute-start | bytes 98312
  187.9 6.2 %collective-permute-start.11 = (bf16[12,1024]{1,0:T(8,128)(2,1)S(1)}, bf16[12,1024]{1,0:T(8,128)(2,1)S(1)}, u32[]{:S(2)}, u32[]{:S(2)}) collective-permute-start(bf16[12,1024]{1,0:T(8,128)(2,1)S(1)} %slice.19), channel_id=1, source_target_pairs={{0,4},{1,5},{2,6},{3,7},{4,8},{5,9},{6,10},{7,11},{8,12},{9,13},{1... | collective-permute-start | bytes 73736
  191.8 17.6 %collective-permute-start.4 = (bf16[16,4096]{1,0:T(8,128)(2,1)S(1)}, bf16[16,4096]{1,0:T(8,128)(2,1)S(1)}, u32[]{:S(2)}, u32[]{:S(2)}) collective-permute-start(bf16[16,4096]{1,0:T(8,128)(2,1)S(1)} %get-tuple-element.69), channel_id=1, source_target_pairs={{0,1},{1,2},{2,3},{3,4},{4,5},{5,6},{6,7},{7,8},{8,9},{9,10},{10,1... | collective-permute-start | bytes 393224
  194.1 15.2 %collective-permute-start.5 = (bf16[16,4096]{1,0:T(8,128)(2,1)S(1)}, bf16[16,4096]{1,0:T(8,128)(2,1)S(1)}, u32[]{:S(2)}, u32[]{:S(2)}) collective-permute-start(bf16[16,4096]{1,0:T(8,128)(2,1)S(1)} %get-tuple-element.69), channel_id=1, source_target_pairs={{0,2},{1,3},{2,4},{3,5},{4,6},{5,7},{6,8},{7,9},{8,10},{9,11},{10,... | collective-permute-start | bytes 393224
  196.2 13.1 %collective-permute-start.6 = (bf16[16,4096]{1,0:T(8,128)(2,1)S(1)}, bf16[16,4096]{1,0:T(8,128)(2,1)S(1)}, u32[]{:S(2)}, u32[]{:S(2)}) collective-permute-start(bf16[16,4096]{1,0:T(8,128)(2,1)S(1)} %get-tuple-element.69), channel_id=1, source_target_pairs={{0,3},{1,4},{2,5},{3,6},{4,7},{5,8},{6,9},{7,10},{8,11},{9,12},{10... | collective-permute-start | bytes 393224
  200.1 9.3 %collective-permute-start.7 = (bf16[12,4096]{1,0:T(8,128)(2,1)S(1)}, bf16[12,4096]{1,0:T(8,128)(2,1)S(1)}, u32[]{:S(2)}, u32[]{:S(2)}) collective-permute-start(bf16[12,4096]{1,0:T(8,128)(2,1)S(1)} %slice.18), channel_id=1, source_target_pairs={{0,4},{1,5},{2,6},{3,7},{4,8},{5,9},{6,10},{7,11},{8,12},{9,13},{1... | collective-permute-start | bytes 294920
Sparse Core Ops, SparseCore 0:
  30.0 59.5 all-gather.8
  92.3 49.7 all-gather.6

commit v3 on v2

--- a/solution.py
+++ b/solution.py
@@ -68,6 +68,8 @@
     lr, lc = latent_proj.shape
     wbuf = jnp.concatenate([patch_proj.reshape(-1), latent_proj.reshape(-1)])
     wbuf = lax.all_gather(wbuf, "x", axis=0)
+    cot_all = lax.all_gather(latent_cotangent, BYTE_AXES, axis=1, tiled=True)
+    wbuf, cot_all = lax.optimization_barrier((wbuf, cot_all))
     wbuf = lax.all_gather(wbuf, "y", axis=0)
     ndp = wbuf.shape[0] * wbuf.shape[1]
     wbuf = wbuf.reshape(ndp, -1)
@@ -83,7 +85,6 @@
         scatter_dimension=0,
         tiled=True,
     )
-    cot_all = lax.all_gather(latent_cotangent, BYTE_AXES, axis=1, tiled=True)
     back = lax.dot_general(
         cot_all[0], latent_row_list, (((1,), (1,)), ((), ())), preferred_element_type=jnp.float32
     )

time: 219 us -> 209 us (0.954)
  starting transfers between devices: 50.9 us -> 44.8 us
    all_gather x1, waiting for transfers between devices: 32.4 us -> 17 us  [per_device(): cot_all = lax.all_gather(latent_cotangent, BYTE_AXES, axis=1, tiled=True)]
    all_gather x1, waiting for transfers between devices: 0.02 us -> 15 us  [per_device(): wbuf = lax.all_gather(wbuf, 'y', axis=0)]
    all_gather x1, blocking collectives: 24 us -> 17 us  [per_device(): patches = lax.all_gather(pooled[None], BYTE_AXES, axis=1, tiled=True)]
    ppermute x4, starting transfers between devices: 25 us -> 19 us  [shifted(): return lax.ppermute(shard, axis, pairs)]
    unnamed x1, blocking collectives: 27.5 us -> 32 us
  transfers between devices with their start and end apart: 14 -> 14, of which waited for: 3 -> 3; matrix products, arithmetic and copies ran while one was open for 14% -> 9% of each run, Pallas kernels for 0% -> 0%
where the time goes in v3:
time: 209 us
  blocking collectives  69.5 us (33%)
  starting transfers between devices  44.8 us (21%)
  waiting for transfers between devices  38.3 us (18%)
  local copies, waits for them, and re-layouts  21.6 us (10%)
  matrix products  17.5 us (8%)
  between operations  15.1 us (7%)
    unnamed x1, blocking collectives  32 us
    unnamed x8, starting transfers between devices  25.7 us
    all_gather x1, blocking collectives, per_device(): wbuf = lax.all_gather(wbuf, 'x', axis=0)  20.5 us
    ppermute x4, starting transfers between devices, shifted(): return lax.ppermute(shard, axis, pairs)  19 us
    all_gather x1, blocking collectives, per_device(): patches = lax.all_gather(pooled[None], BYTE_AXES, axis=1, tiled=True)  17 us
    all_gather x1, waiting for transfers between devices, per_device(): cot_all = lax.all_gather(latent_cotangent, BYTE_AXES, axis=1, tiled=True)  17 us
    all_gather x1, waiting for transfers between devices, per_device(): wbuf = lax.all_gather(wbuf, 'y', axis=0)  15 us
    unnamed x20, local copies, waits for them, and re-layouts  7.17 us
  transfers between devices with their start and end apart: 14, of which 3 were waited for; matrix products, arithmetic and copies ran while one was open for 9% of the time, Pallas kernels for 0%

profile of v3, /device:TPU:129, one launch (start us, length us, event | category | flops | bytes accessed | tf_op | source)
XLA Modules:
  0.0 208.5 jit_solution(11737477219414455751)
XLA Ops:
  7.3 1.8 copy.53
  9.2 4.9 %collective-permute-start = (bf16[1,128,1024]{2,1,0:T(8,128)(2,1)}, bf16[1,128,1024]{2,1,0:T(8,128)(2,1)S(1)}, u32[]{:S(2)}, u32[]{:S(2)}) collective-permute-start(bf16[1,128,1024]{2,1,0:T(8,128)(2,1)} %param.11), channel_id=1, source_target_pairs={{0,2},{1,3},{2,4},{3,5},{4,6},{5,7},{6,8},{7,9},{8,10},{9,11},{10,... | collective-permute-start | bytes 786440 | tf_op jit(solution)/shard_map/ppermute | solution.py:18
  14.1 5.8 %collective-permute-start.1 = (bf16[1,128,1024]{2,1,0:T(8,128)(2,1)}, bf16[1,128,1024]{2,1,0:T(8,128)(2,1)S(1)}, u32[]{:S(2)}, u32[]{:S(2)}) collective-permute-start(bf16[1,128,1024]{2,1,0:T(8,128)(2,1)} %param.11), channel_id=1, source_target_pairs={{0,1},{1,2},{2,3},{3,4},{4,5},{5,6},{6,7},{7,8},{8,9},{9,10},{10,1... | collective-permute-start | bytes 786440 | tf_op jit(solution)/shard_map/ppermute | solution.py:18
  19.8 6.1 %collective-permute-start.2 = (bf16[1,128,1024]{2,1,0:T(8,128)(2,1)}, bf16[1,128,1024]{2,1,0:T(8,128)(2,1)S(1)}, u32[]{:S(2)}, u32[]{:S(2)}) collective-permute-start(bf16[1,128,1024]{2,1,0:T(8,128)(2,1)} %param.10), channel_id=1, source_target_pairs={{0,2},{1,3},{2,4},{3,5},{4,6},{5,7},{6,8},{7,9},{8,10},{9,11},{10,... | collective-permute-start | bytes 786440 | tf_op jit(solution)/shard_map/ppermute | solution.py:18
  26.0 2.2 %collective-permute-start.3 = (bf16[1,128,1024]{2,1,0:T(8,128)(2,1)}, bf16[1,128,1024]{2,1,0:T(8,128)(2,1)S(1)}, u32[]{:S(2)}, u32[]{:S(2)}) collective-permute-start(bf16[1,128,1024]{2,1,0:T(8,128)(2,1)} %param.10), channel_id=1, source_target_pairs={{0,1},{1,2},{2,3},{3,4},{4,5},{5,6},{6,7},{7,8},{8,9},{9,10},{10,1... | collective-permute-start | bytes 786440 | tf_op jit(solution)/shard_map/ppermute | solution.py:18
  29.9 20.5 %all-gather.1 = bf16[163840]{0:T(1024)(128)(2,1)S(1)} all-gather(bf16[20480]{0:T(1024)(128)(2,1)S(1)} %pad_maximum_fusion), channel_id=3, replica_groups=mesh['y'=8,'x'=8,'z'=8,'c'=2] {'x'}, dimensions={0}, use_global_device_ids=true | all-gather | bytes 368640 | tf_op jit(solution)/shard_map/all_gather | solution.py:70
  51.3 17.0 %all-gather.7.cloned.1.call-done = bf16[1,192,4096]{2,0,1:T(2,128)(2,1)} async-done(((bf16[1,12,4096]{2,0,1:T(2,128)(2,1)}), bf16[1,192,4096]{2,0,1:T(2,128)(2,1)}) %all-gather.7.cloned.1.call-update) | async-done | bytes 1572880 | tf_op jit(solution)/shard_map/all_gather | solution.py:71
  70.2 10.5 %while.11 = (s32[]{:T(128)}, bf16[4,128,4,64]{1,3,2,0:T(8,128)(2,1)}, bf16[4,384,4,64]{1,3,2,0:T(8,128)(2,1)S(1)}, bf16[4,128,4,64]{1,3,2,0:T(8,128)(2,1)S(1)}, ...) while((s32[]{:T(128)}, ...), condition=%wide.region_3.4_spmd.clone, body=%wide.region_0.3_spmd.clone.sunk | while | flops 77497600 | bytes 3301333 | solution.py:57
  71.2 1.7 fusion.95
  73.8 1.7 fusion.95
  76.4 1.7 fusion.95
  79.0 1.7 fusion.95
  80.7 1.1 fusion.46
  81.8 17.0 %all-gather.3 = bf16[16,12,1024]{2,1,0:T(8,128)(2,1)S(1)} all-gather(bf16[1,12,1024]{2,1,0:T(8,128)(2,1)S(1)} %fusion.46), channel_id=2, replica_groups=mesh['y'=8,'x'=8,'z'=8,'c'=2] {'z','c'}, dimensions={0}, use_global_device_ids=true | all-gather | bytes 417792 | tf_op jit(solution)/shard_map/all_gather | solution.py:78
  99.0 15.0 %all-gather.9.cloned.1.call-done = bf16[64,20480]{1,0:T(8,128)(2,1)} async-done(((bf16[8,20480]{1,0:T(8,128)(2,1)}), bf16[64,20480]{1,0:T(8,128)(2,1)}) %all-gather.9.cloned.1.call-update) | async-done | bytes 2621456 | tf_op jit(solution)/shard_map/all_gather | solution.py:73
  115.3 1.6 slice-done
  116.9 5.5 %reshape.82 = bf16[64,256,64]{2,1,0:T(8,128)(2,1)} reshape(bf16[64,16384]{1,0:T(8,128)(2,1)S(1)} %slice-done) | data formatting | bytes 4194304 | tf_op jit(solution)/shard_map/reshape | solution.py:77
  122.4 3.5 %copy.54 = bf16[256,64,64]{0,2,1:T(8,128)(2,1)S(1)} copy(bf16[256,64,64]{2,0,1:T(8,128)(2,1)} %bitcast.92) | data formatting | bytes 4194304 | tf_op jit(solution)/shard_map/transpose | solution.py:77
  126.2 2.0 convolution_convert_fusion.1
  128.2 4.1 %convolution_convert_fusion.2 = bf16[192,1024]{1,0:T(8,128)(2,1)S(1)} fusion(bf16[1024,256]{1,0:T(8,128)(2,1)S(1)} %reshape.81, bf16[256,4096]{0,1:T(8,128)(2,1)S(1)} %bitcast.94, bf16[1,192,4096]{2,0,1:T(2,128)(2,1)} %all-gather.7.cloned.1.call-done, f32[192,256]{1,0:T(8,128)S(1)} %fusion.68), kind=kOutput, calls=%fused_computation.32 | convolution fusion | flops 503955456 | bytes 4784128 | tf_op jit(solution)/shard_map/dot_general | solution.py:95
  132.3 32.0 %fusion.62 = (bf16[16,4096]{1,0:T(8,128)(2,1)S(1)}, bf16[16,1024]{1,0:T(8,128)(2,1)S(1)}) fusion(bf16[192,4096]{1,0:T(8,128)(2,1)} %convolution_convert_fusion.1, bf16[192,1024]{1,0:T(8,128)(2,1)S(1)} %convolution_convert_fusion.2), kind=kCustom, calls=%all-reduce-scatter.2 | all-reduce-scatter fusion | flops 1310721 | bytes 2134016
  164.3 5.5 %collective-permute-start.10 = (bf16[16,1024]{1,0:T(8,128)(2,1)S(1)}, bf16[16,1024]{1,0:T(8,128)(2,1)S(1)}, u32[]{:S(2)}, u32[]{:S(2)}) collective-permute-start(bf16[16,1024]{1,0:T(8,128)(2,1)S(1)} %get-tuple-element.74), channel_id=1, source_target_pairs={{0,3},{1,4},{2,5},{3,6},{4,7},{5,8},{6,9},{7,10},{8,11},{9,12},{10... | collective-permute-start | bytes 98312
  169.8 3.6 %collective-permute-start.8 = (bf16[16,1024]{1,0:T(8,128)(2,1)S(1)}, bf16[16,1024]{1,0:T(8,128)(2,1)S(1)}, u32[]{:S(2)}, u32[]{:S(2)}) collective-permute-start(bf16[16,1024]{1,0:T(8,128)(2,1)S(1)} %get-tuple-element.74), channel_id=1, source_target_pairs={{0,1},{1,2},{2,3},{3,4},{4,5},{5,6},{6,7},{7,8},{8,9},{9,10},{10,1... | collective-permute-start | bytes 98312
  173.3 4.9 %collective-permute-start.9 = (bf16[16,1024]{1,0:T(8,128)(2,1)S(1)}, bf16[16,1024]{1,0:T(8,128)(2,1)S(1)}, u32[]{:S(2)}, u32[]{:S(2)}) collective-permute-start(bf16[16,1024]{1,0:T(8,128)(2,1)S(1)} %get-tuple-element.74), channel_id=1, source_target_pairs={{0,2},{1,3},{2,4},{3,5},{4,6},{5,7},{6,8},{7,9},{8,10},{9,11},{10,... | collective-permute-start | bytes 98312
  178.3 1.9 collective-permute-start.11
  180.2 1.3 dynamic-slice.6
  182.2 2.3 %collective-permute-start.4 = (bf16[16,4096]{1,0:T(8,128)(2,1)S(1)}, bf16[16,4096]{1,0:T(8,128)(2,1)S(1)}, u32[]{:S(2)}, u32[]{:S(2)}) collective-permute-start(bf16[16,4096]{1,0:T(8,128)(2,1)S(1)} %get-tuple-element.73), channel_id=1, source_target_pairs={{0,1},{1,2},{2,3},{3,4},{4,5},{5,6},{6,7},{7,8},{8,9},{9,10},{10,1... | collective-permute-start | bytes 393224
  184.5 2.1 %collective-permute-start.5 = (bf16[16,4096]{1,0:T(8,128)(2,1)S(1)}, bf16[16,4096]{1,0:T(8,128)(2,1)S(1)}, u32[]{:S(2)}, u32[]{:S(2)}) collective-permute-start(bf16[16,4096]{1,0:T(8,128)(2,1)S(1)} %get-tuple-element.73), channel_id=1, source_target_pairs={{0,2},{1,3},{2,4},{3,5},{4,6},{5,7},{6,8},{7,9},{8,10},{9,11},{10,... | collective-permute-start | bytes 393224
  186.6 3.8 %collective-permute-start.6 = (bf16[16,4096]{1,0:T(8,128)(2,1)S(1)}, bf16[16,4096]{1,0:T(8,128)(2,1)S(1)}, u32[]{:S(2)}, u32[]{:S(2)}) collective-permute-start(bf16[16,4096]{1,0:T(8,128)(2,1)S(1)} %get-tuple-element.73), channel_id=1, source_target_pairs={{0,3},{1,4},{2,5},{3,6},{4,7},{5,8},{6,9},{7,10},{8,11},{9,12},{10... | collective-permute-start | bytes 393224
  190.5 1.6 collective-permute-start.7
  193.4 6.3 %collective-permute-done.7 = bf16[12,4096]{1,0:T(8,128)(2,1)S(1)} collective-permute-done((bf16[12,4096]{1,0:T(8,128)(2,1)S(1)}, bf16[12,4096]{1,0:T(8,128)(2,1)S(1)}, u32[]{:S(2)}, u32[]{:S(2)}) %collective-permute-start.7) | collective-permute-done | bytes 98336
  199.8 1.2 concatenate.36
  (66 shorter events, 11.9 us)
Async XLA Ops:
  7.2 61.7 %copy-start.1 = (bf16[1,128,1024]{2,1,0:T(8,128)(2,1)S(1)}, bf16[1,128,1024]{2,1,0:T(8,128)(2,1)}, u32[]{:S(2)}) copy-start(bf16[1,128,1024]{2,1,0:T(8,128)(2,1)} %param.11) | copy-start | bytes 786436
  7.2 61.5 %copy-start.2 = (bf16[1,128,1024]{2,1,0:T(8,128)(2,1)S(1)}, bf16[1,128,1024]{2,1,0:T(8,128)(2,1)}, u32[]{:S(2)}) copy-start(bf16[1,128,1024]{2,1,0:T(8,128)(2,1)} %param.10) | copy-start | bytes 786436
  7.2 61.1 %copy-start.3 = (s32[1,1,12]{2,1,0:T(1,128)S(1)}, s32[1,1,12]{2,1,0:T(1,128)}, u32[]{:S(2)}) copy-start(s32[1,1,12]{2,1,0:T(1,128)} %param.12) | copy-start | bytes 148
  7.2 61.9 %copy-start = (bf16[1,128,1024]{2,1,0:T(8,128)(2,1)S(1)}, bf16[1,128,1024]{2,1,0:T(8,128)(2,1)}, u32[]{:S(2)}) copy-start(bf16[1,128,1024]{2,1,0:T(8,128)(2,1)} %param.9) | copy-start | bytes 786436
  7.2 61.1 %all-gather.7.cloned.1.call-start = ((), (), s32[]{:S(2)}) async-start(), calls=%async_computation | async-start | bytes 3342336 | tf_op jit(solution)/shard_map/all_gather | solution.py:71
  9.1 104.8 %all-gather.9.cloned.1.call-start = ((), (), s32[]{:S(2)}) async-start(), calls=%async_computation.1 | async-start | bytes 2949120 | tf_op jit(solution)/shard_map/all_gather | solution.py:73
  9.2 60.1 %collective-permute-start = (bf16[1,128,1024]{2,1,0:T(8,128)(2,1)}, bf16[1,128,1024]{2,1,0:T(8,128)(2,1)S(1)}, u32[]{:S(2)}, u32[]{:S(2)}) collective-permute-start(bf16[1,128,1024]{2,1,0:T(8,128)(2,1)} %param.11), channel_id=1, source_target_pairs={{0,2},{1,3},{2,4},{3,5},{4,6},{5,7},{6,8},{7,9},{8,10},{9,11},{10,... | collective-permute-start | bytes 786440 | tf_op jit(solution)/shard_map/ppermute | solution.py:18
  14.1 55.4 %collective-permute-start.1 = (bf16[1,128,1024]{2,1,0:T(8,128)(2,1)}, bf16[1,128,1024]{2,1,0:T(8,128)(2,1)S(1)}, u32[]{:S(2)}, u32[]{:S(2)}) collective-permute-start(bf16[1,128,1024]{2,1,0:T(8,128)(2,1)} %param.11), channel_id=1, source_target_pairs={{0,1},{1,2},{2,3},{3,4},{4,5},{5,6},{6,7},{7,8},{8,9},{9,10},{10,1... | collective-permute-start | bytes 786440 | tf_op jit(solution)/shard_map/ppermute | solution.py:18
  19.8 49.8 %collective-permute-start.2 = (bf16[1,128,1024]{2,1,0:T(8,128)(2,1)}, bf16[1,128,1024]{2,1,0:T(8,128)(2,1)S(1)}, u32[]{:S(2)}, u32[]{:S(2)}) collective-permute-start(bf16[1,128,1024]{2,1,0:T(8,128)(2,1)} %param.10), channel_id=1, source_target_pairs={{0,2},{1,3},{2,4},{3,5},{4,6},{5,7},{6,8},{7,9},{8,10},{9,11},{10,... | collective-permute-start | bytes 786440 | tf_op jit(solution)/shard_map/ppermute | solution.py:18
  26.0 43.8 %collective-permute-start.3 = (bf16[1,128,1024]{2,1,0:T(8,128)(2,1)}, bf16[1,128,1024]{2,1,0:T(8,128)(2,1)S(1)}, u32[]{:S(2)}, u32[]{:S(2)}) collective-permute-start(bf16[1,128,1024]{2,1,0:T(8,128)(2,1)} %param.10), channel_id=1, source_target_pairs={{0,1},{1,2},{2,3},{3,4},{4,5},{5,6},{6,7},{7,8},{8,9},{9,10},{10,1... | collective-permute-start | bytes 786440 | tf_op jit(solution)/shard_map/ppermute | solution.py:18
  115.3 1.6 slice-start
  164.3 22.3 %collective-permute-start.10 = (bf16[16,1024]{1,0:T(8,128)(2,1)S(1)}, bf16[16,1024]{1,0:T(8,128)(2,1)S(1)}, u32[]{:S(2)}, u32[]{:S(2)}) collective-permute-start(bf16[16,1024]{1,0:T(8,128)(2,1)S(1)} %get-tuple-element.74), channel_id=1, source_target_pairs={{0,3},{1,4},{2,5},{3,6},{4,7},{5,8},{6,9},{7,10},{8,11},{9,12},{10... | collective-permute-start | bytes 98312
  169.8 20.7 %collective-permute-start.8 = (bf16[16,1024]{1,0:T(8,128)(2,1)S(1)}, bf16[16,1024]{1,0:T(8,128)(2,1)S(1)}, u32[]{:S(2)}, u32[]{:S(2)}) collective-permute-start(bf16[16,1024]{1,0:T(8,128)(2,1)S(1)} %get-tuple-element.74), channel_id=1, source_target_pairs={{0,1},{1,2},{2,3},{3,4},{4,5},{5,6},{6,7},{7,8},{8,9},{9,10},{10,1... | collective-permute-start | bytes 98312
  173.3 18.8 %collective-permute-start.9 = (bf16[16,1024]{1,0:T(8,128)(2,1)S(1)}, bf16[16,1024]{1,0:T(8,128)(2,1)S(1)}, u32[]{:S(2)}, u32[]{:S(2)}) collective-permute-start(bf16[16,1024]{1,0:T(8,128)(2,1)S(1)} %get-tuple-element.74), channel_id=1, source_target_pairs={{0,2},{1,3},{2,4},{3,5},{4,6},{5,7},{6,8},{7,9},{8,10},{9,11},{10,... | collective-permute-start | bytes 98312
  178.3 6.2 %collective-permute-start.11 = (bf16[12,1024]{1,0:T(8,128)(2,1)S(1)}, bf16[12,1024]{1,0:T(8,128)(2,1)S(1)}, u32[]{:S(2)}, u32[]{:S(2)}) collective-permute-start(bf16[12,1024]{1,0:T(8,128)(2,1)S(1)} %slice.19), channel_id=1, source_target_pairs={{0,4},{1,5},{2,6},{3,7},{4,8},{5,9},{6,10},{7,11},{8,12},{9,13},{1... | collective-permute-start | bytes 73736
  182.2 17.6 %collective-permute-start.4 = (bf16[16,4096]{1,0:T(8,128)(2,1)S(1)}, bf16[16,4096]{1,0:T(8,128)(2,1)S(1)}, u32[]{:S(2)}, u32[]{:S(2)}) collective-permute-start(bf16[16,4096]{1,0:T(8,128)(2,1)S(1)} %get-tuple-element.73), channel_id=1, source_target_pairs={{0,1},{1,2},{2,3},{3,4},{4,5},{5,6},{6,7},{7,8},{8,9},{9,10},{10,1... | collective-permute-start | bytes 393224
  184.5 15.2 %collective-permute-start.5 = (bf16[16,4096]{1,0:T(8,128)(2,1)S(1)}, bf16[16,4096]{1,0:T(8,128)(2,1)S(1)}, u32[]{:S(2)}, u32[]{:S(2)}) collective-permute-start(bf16[16,4096]{1,0:T(8,128)(2,1)S(1)} %get-tuple-element.73), channel_id=1, source_target_pairs={{0,2},{1,3},{2,4},{3,5},{4,6},{5,7},{6,8},{7,9},{8,10},{9,11},{10,... | collective-permute-start | bytes 393224
  186.6 13.1 %collective-permute-start.6 = (bf16[16,4096]{1,0:T(8,128)(2,1)S(1)}, bf16[16,4096]{1,0:T(8,128)(2,1)S(1)}, u32[]{:S(2)}, u32[]{:S(2)}) collective-permute-start(bf16[16,4096]{1,0:T(8,128)(2,1)S(1)} %get-tuple-element.73), channel_id=1, source_target_pairs={{0,3},{1,4},{2,5},{3,6},{4,7},{5,8},{6,9},{7,10},{8,11},{9,12},{10... | collective-permute-start | bytes 393224
  190.5 9.3 %collective-permute-start.7 = (bf16[12,4096]{1,0:T(8,128)(2,1)S(1)}, bf16[12,4096]{1,0:T(8,128)(2,1)S(1)}, u32[]{:S(2)}, u32[]{:S(2)}) collective-permute-start(bf16[12,4096]{1,0:T(8,128)(2,1)S(1)} %slice.18), channel_id=1, source_target_pairs={{0,4},{1,5},{2,6},{3,7},{4,8},{5,9},{6,10},{7,11},{8,12},{9,13},{1... | collective-permute-start | bytes 294920
Sparse Core Ops, SparseCore 0:
  10.7 57.4 all-gather.6
  70.9 42.9 all-gather.8

commit v4 on v3

--- a/solution.py
+++ b/solution.py
@@ -78,13 +78,22 @@
     patches = lax.all_gather(pooled[None], BYTE_AXES, axis=1, tiled=True)
     hidden_in = jnp.dot(patches[0], proj_cols, preferred_element_type=jnp.float32)
     activation = jax.nn.silu(hidden_in).astype(jnp.bfloat16)
+    shards = patches.shape[1] // pooled.shape[0]
+    rows_of = pooled.shape[0]
+    rows_pad = -(-rows_of // 8) * 8
+
+    def padded(block_product):
+        split = block_product.reshape(shards, rows_of, -1)
+        split = jnp.pad(split, ((0, 0), (0, rows_pad - rows_of), (0, 0)))
+        return split.reshape(shards * rows_pad, -1)
+
     piece = activation
     latent = lax.psum_scatter(
-        jnp.dot(piece, latent_row_list, preferred_element_type=jnp.float32).astype(jnp.bfloat16),
+        padded(jnp.dot(piece, latent_row_list, preferred_element_type=jnp.float32).astype(jnp.bfloat16)),
         BYTE_AXES,
         scatter_dimension=0,
         tiled=True,
-    )
+    )[:rows_of]
     back = lax.dot_general(
         cot_all[0], latent_row_list, (((1,), (1,)), ((), ())), preferred_element_type=jnp.float32
     )
@@ -92,13 +101,13 @@
     act_grad = (back * sigma * (1.0 + hidden_in * (1.0 - sigma))).astype(jnp.bfloat16)
     piece = act_grad
     grads = lax.psum_scatter(
-        lax.dot_general(
+        padded(lax.dot_general(
             piece, proj_cols, (((1,), (1,)), ((), ())), preferred_element_type=jnp.float32
-        ).astype(jnp.bfloat16),
+        ).astype(jnp.bfloat16)),
         BYTE_AXES,
         scatter_dimension=0,
         tiled=True,
-    ).astype(jnp.float32)
+    )[:rows_of].astype(jnp.float32)
     grads = jnp.where(valid[:, None], grads, 0.0)
     return (latent[None], grads.astype(jnp.bfloat16)[None])
 

time: 209 us -> 275 us (1.32)
  the two profiles are of different devices: /device:TPU:129 before, /device:TPU:4 now
where the time goes in v4:
time: 275 us
  waiting for transfers between devices  156 us (57%)
  blocking collectives  43.3 us (16%)
  local copies, waits for them, and re-layouts  24.2 us (9%)
  starting transfers between devices  17.5 us (6%)
  matrix products  17.4 us (6%)
  between operations  14.1 us (5%)
    reduce_scatter x1, waiting for transfers between devices, per_device(): lax.psum_scatter(padded(jnp.dot(piece, latent_row_list, preferred_element...  66 us
    reduce_scatter x1, waiting for transfers between devices, per_device(): lax.psum_scatter(padded(lax.dot_general(piece, proj_cols, (((1,), (1,)),...  57.4 us
    all_gather x1, blocking collectives, per_device(): wbuf = lax.all_gather(wbuf, 'x', axis=0)  25.9 us
    all_gather x1, blocking collectives, per_device(): patches = lax.all_gather(pooled[None], BYTE_AXES, axis=1, tiled=True)  17.5 us
    ppermute x4, starting transfers between devices, shifted(): return lax.ppermute(shard, axis, pairs)  17.3 us
    all_gather x1, waiting for transfers between devices, per_device(): wbuf = lax.all_gather(wbuf, 'y', axis=0)  16.7 us
    all_gather x1, waiting for transfers between devices, per_device(): cot_all = lax.all_gather(latent_cotangent, BYTE_AXES, axis=1, tiled=True)  15.5 us
    dot_general x4, matrix products, attend(): jnp.einsum('hij,jhd->ihd', weights, values, preferred_element_type=jnp.fl...  6.67 us
  transfers between devices with their start and end apart: 8, of which 4 were waited for; matrix products, arithmetic and copies ran while one was open for 8% of the time, Pallas kernels for 0%

profile of v4, /device:TPU:4, one launch (start us, length us, event | category | flops | bytes accessed | tf_op | source)
XLA Modules:
  0.0 274.7 jit_solution(4939947336698451842)
XLA Ops:
  7.3 1.8 copy.53
  9.1 5.2 %collective-permute-start = (bf16[1,128,1024]{2,1,0:T(8,128)(2,1)}, bf16[1,128,1024]{2,1,0:T(8,128)(2,1)S(1)}, u32[]{:S(2)}, u32[]{:S(2)}) collective-permute-start(bf16[1,128,1024]{2,1,0:T(8,128)(2,1)} %param.11), channel_id=1, source_target_pairs={{0,2},{1,3},{2,4},{3,5},{4,6},{5,7},{6,8},{7,9},{8,10},{9,11},{10,... | collective-permute-start | bytes 786440 | tf_op jit(solution)/shard_map/ppermute | solution.py:18
  14.4 1.5 collective-permute-start.1
  15.8 5.6 %collective-permute-start.2 = (bf16[1,128,1024]{2,1,0:T(8,128)(2,1)}, bf16[1,128,1024]{2,1,0:T(8,128)(2,1)S(1)}, u32[]{:S(2)}, u32[]{:S(2)}) collective-permute-start(bf16[1,128,1024]{2,1,0:T(8,128)(2,1)} %param.10), channel_id=1, source_target_pairs={{0,2},{1,3},{2,4},{3,5},{4,6},{5,7},{6,8},{7,9},{8,10},{9,11},{10,... | collective-permute-start | bytes 786440 | tf_op jit(solution)/shard_map/ppermute | solution.py:18
  21.5 5.0 %collective-permute-start.3 = (bf16[1,128,1024]{2,1,0:T(8,128)(2,1)}, bf16[1,128,1024]{2,1,0:T(8,128)(2,1)S(1)}, u32[]{:S(2)}, u32[]{:S(2)}) collective-permute-start(bf16[1,128,1024]{2,1,0:T(8,128)(2,1)} %param.10), channel_id=1, source_target_pairs={{0,1},{1,2},{2,3},{3,4},{4,5},{5,6},{6,7},{7,8},{8,9},{9,10},{10,1... | collective-permute-start | bytes 786440 | tf_op jit(solution)/shard_map/ppermute | solution.py:18
  26.5 0.9 copy.52
  27.5 0.7 copy.56
  28.2 25.9 %all-gather.1 = bf16[163840]{0:T(1024)(128)(2,1)S(1)} all-gather(bf16[20480]{0:T(1024)(128)(2,1)S(1)} %pad_maximum_fusion), channel_id=3, replica_groups=mesh['y'=8,'x'=8,'z'=8,'c'=2] {'x'}, dimensions={0}, use_global_device_ids=true | all-gather | bytes 368640 | tf_op jit(solution)/shard_map/all_gather | solution.py:70
  54.1 0.9 reshape.101
  55.0 15.5 %all-gather.7.cloned.1.call-done = bf16[1,192,4096]{2,0,1:T(2,128)(2,1)} async-done(((bf16[1,12,4096]{2,0,1:T(2,128)(2,1)}), bf16[1,192,4096]{2,0,1:T(2,128)(2,1)}) %all-gather.7.cloned.1.call-update) | async-done | bytes 1572880 | tf_op jit(solution)/shard_map/all_gather | solution.py:71
  72.4 10.4 %while.11 = (s32[]{:T(128)}, bf16[4,128,4,64]{1,3,2,0:T(8,128)(2,1)}, bf16[4,384,4,64]{1,3,2,0:T(8,128)(2,1)S(1)}, bf16[4,128,4,64]{1,3,2,0:T(8,128)(2,1)S(1)}, ...) while((s32[]{:T(128)}, ...), condition=%wide.region_3.4_spmd.clone, body=%wide.region_0.3_spmd.clone.sunk | while | flops 77497600 | bytes 3301333 | solution.py:57
  72.9 0.5 fusion.90
  73.4 1.7 fusion.92
  76.0 1.7 fusion.92
  78.6 1.7 fusion.92
  81.2 1.7 fusion.92
  82.9 1.1 fusion.44
  84.0 17.5 %all-gather.3 = bf16[16,12,1024]{2,1,0:T(8,128)(2,1)S(1)} all-gather(bf16[1,12,1024]{2,1,0:T(8,128)(2,1)S(1)} %fusion.44), channel_id=2, replica_groups=mesh['y'=8,'x'=8,'z'=8,'c'=2] {'z','c'}, dimensions={0}, use_global_device_ids=true | all-gather | bytes 417792 | tf_op jit(solution)/shard_map/all_gather | solution.py:78
  101.6 16.7 %all-gather.9.cloned.1.call-done = bf16[64,20480]{1,0:T(8,128)(2,1)} async-done(((bf16[8,20480]{1,0:T(8,128)(2,1)}), bf16[64,20480]{1,0:T(8,128)(2,1)}) %all-gather.9.cloned.1.call-update) | async-done | bytes 2621456 | tf_op jit(solution)/shard_map/all_gather | solution.py:73
  118.3 1.1 slice.24
  119.6 1.6 slice-done
  121.2 5.5 %reshape.94 = bf16[64,256,64]{2,1,0:T(8,128)(2,1)} reshape(bf16[64,16384]{1,0:T(8,128)(2,1)S(1)} %slice-done) | data formatting | bytes 4194304 | tf_op jit(solution)/shard_map/reshape | solution.py:77
  126.7 3.5 %copy.54 = bf16[256,64,64]{0,2,1:T(8,128)(2,1)S(1)} copy(bf16[256,64,64]{2,0,1:T(8,128)(2,1)} %bitcast.88) | data formatting | bytes 4194304 | tf_op jit(solution)/shard_map/transpose | solution.py:77
  130.6 4.1 %convolution_convert_fusion.2 = bf16[192,1024]{1,0:T(8,128)(2,1)S(1)} fusion(bf16[1024,256]{1,0:T(8,128)(2,1)S(1)} %reshape.93, bf16[256,4096]{0,1:T(8,128)(2,1)S(1)} %bitcast.89, bf16[1,192,4096]{2,0,1:T(2,128)(2,1)} %all-gather.7.cloned.1.call-done, f32[192,256]{1,0:T(8,128)S(1)} %fusion.65), kind=kOutput, calls=%fused_computation.32 | convolution fusion | flops 503955456 | bytes 4784128 | tf_op jit(solution)/shard_map/dot_general | solution.py:104
  134.7 0.9 pad.9
  135.7 2.0 convolution_convert_fusion.1
  137.7 2.3 reshape.96
  140.0 1.6 pad.8
  141.7 57.4 %reduce-scatter.5.cloned.1.call-done = bf16[16,1024]{1,0:T(8,128)(2,1)} async-done(((bf16[256,1024]{1,0:T(8,128)(2,1)}), bf16[16,1024]{1,0:T(8,128)(2,1)}) %reduce-scatter.5.cloned.1.call-update) | async-done | bytes 32784 | tf_op jit(solution)/shard_map/reduce_scatter | solution.py:103
  199.1 1.4 fusion.50
  200.6 66.0 %reduce-scatter.3.cloned.1.call-done = bf16[16,4096]{1,0:T(8,128)(2,1)} async-done(((bf16[256,4096]{1,0:T(8,128)(2,1)}), bf16[16,4096]{1,0:T(8,128)(2,1)}) %reduce-scatter.3.cloned.1.call-update) | async-done | bytes 131088 | tf_op jit(solution)/shard_map/reduce_scatter | solution.py:91
  266.6 1.6 slice_bitcast_fusion
  (54 shorter events, 6.0 us)
Async XLA Ops:
  7.2 63.9 %copy-start.1 = (bf16[1,128,1024]{2,1,0:T(8,128)(2,1)S(1)}, bf16[1,128,1024]{2,1,0:T(8,128)(2,1)}, u32[]{:S(2)}) copy-start(bf16[1,128,1024]{2,1,0:T(8,128)(2,1)} %param.11) | copy-start | bytes 786436
  7.2 63.7 %copy-start.2 = (bf16[1,128,1024]{2,1,0:T(8,128)(2,1)S(1)}, bf16[1,128,1024]{2,1,0:T(8,128)(2,1)}, u32[]{:S(2)}) copy-start(bf16[1,128,1024]{2,1,0:T(8,128)(2,1)} %param.10) | copy-start | bytes 786436
  7.2 63.3 %copy-start.3 = (s32[1,1,12]{2,1,0:T(1,128)S(1)}, s32[1,1,12]{2,1,0:T(1,128)}, u32[]{:S(2)}) copy-start(s32[1,1,12]{2,1,0:T(1,128)} %param.12) | copy-start | bytes 148
  7.2 64.1 %copy-start = (bf16[1,128,1024]{2,1,0:T(8,128)(2,1)S(1)}, bf16[1,128,1024]{2,1,0:T(8,128)(2,1)}, u32[]{:S(2)}) copy-start(bf16[1,128,1024]{2,1,0:T(8,128)(2,1)} %param.9) | copy-start | bytes 786436
  7.2 63.3 %all-gather.7.cloned.1.call-start = ((), (), s32[]{:S(2)}) async-start(), calls=%async_computation.2 | async-start | bytes 3342336 | tf_op jit(solution)/shard_map/all_gather | solution.py:71
  9.1 109.2 %all-gather.9.cloned.1.call-start = ((), (), s32[]{:S(2)}) async-start(), calls=%async_computation.5 | async-start | bytes 2949120 | tf_op jit(solution)/shard_map/all_gather | solution.py:73
  9.1 62.3 %collective-permute-start = (bf16[1,128,1024]{2,1,0:T(8,128)(2,1)}, bf16[1,128,1024]{2,1,0:T(8,128)(2,1)S(1)}, u32[]{:S(2)}, u32[]{:S(2)}) collective-permute-start(bf16[1,128,1024]{2,1,0:T(8,128)(2,1)} %param.11), channel_id=1, source_target_pairs={{0,2},{1,3},{2,4},{3,5},{4,6},{5,7},{6,8},{7,9},{8,10},{9,11},{10,... | collective-permute-start | bytes 786440 | tf_op jit(solution)/shard_map/ppermute | solution.py:18
  14.4 57.3 %collective-permute-start.1 = (bf16[1,128,1024]{2,1,0:T(8,128)(2,1)}, bf16[1,128,1024]{2,1,0:T(8,128)(2,1)S(1)}, u32[]{:S(2)}, u32[]{:S(2)}) collective-permute-start(bf16[1,128,1024]{2,1,0:T(8,128)(2,1)} %param.11), channel_id=1, source_target_pairs={{0,1},{1,2},{2,3},{3,4},{4,5},{5,6},{6,7},{7,8},{8,9},{9,10},{10,1... | collective-permute-start | bytes 786440 | tf_op jit(solution)/shard_map/ppermute | solution.py:18
  15.8 56.0 %collective-permute-start.2 = (bf16[1,128,1024]{2,1,0:T(8,128)(2,1)}, bf16[1,128,1024]{2,1,0:T(8,128)(2,1)S(1)}, u32[]{:S(2)}, u32[]{:S(2)}) collective-permute-start(bf16[1,128,1024]{2,1,0:T(8,128)(2,1)} %param.10), channel_id=1, source_target_pairs={{0,2},{1,3},{2,4},{3,5},{4,6},{5,7},{6,8},{7,9},{8,10},{9,11},{10,... | collective-permute-start | bytes 786440 | tf_op jit(solution)/shard_map/ppermute | solution.py:18
  21.5 50.5 %collective-permute-start.3 = (bf16[1,128,1024]{2,1,0:T(8,128)(2,1)}, bf16[1,128,1024]{2,1,0:T(8,128)(2,1)S(1)}, u32[]{:S(2)}, u32[]{:S(2)}) collective-permute-start(bf16[1,128,1024]{2,1,0:T(8,128)(2,1)} %param.10), channel_id=1, source_target_pairs={{0,1},{1,2},{2,3},{3,4},{4,5},{5,6},{6,7},{7,8},{8,9},{9,10},{10,1... | collective-permute-start | bytes 786440 | tf_op jit(solution)/shard_map/ppermute | solution.py:18
  70.5 128.6 %reduce-scatter.5.cloned.1.call-start = ((), (), s32[]{:S(2)}) async-start(), calls=%async_computation.4 | async-start | bytes 557056 | tf_op jit(solution)/shard_map/reduce_scatter | solution.py:103
  119.6 1.6 slice-start
  135.6 131.0 %reduce-scatter.3.cloned.1.call-start = ((), (), s32[]{:S(2)}) async-start(), calls=%async_computation.3 | async-start | bytes 2228224 | tf_op jit(solution)/shard_map/reduce_scatter | solution.py:91
Sparse Core Ops, SparseCore 0:
  10.7 59.6 all-gather.6
  73.1 45.1 all-gather.8
  135.8 63.3 reduce-scatter.4
  202.8 63.8 reduce-scatter.2
